TPU v7x, 512 devices: a whole 4x8x8 slice. The times are simulated.
512 devices in a mesh: rep: 32 (over z_hi, x, core), exp: 16 (over y, z_lo).
Axes of the slice: x: 4, y: 8, z: 8 (z_hi: 4, z_lo: 2; z = z_hi * 2 + z_lo), core: 2. Of those that a mesh axis runs over, the one named last changes fastest.
Arguments:
- tokens: bfloat16 [65536, 2048], P(('rep', 'exp')), may hold values from -6 to 6
- expert_ids: int32 [65536, 8], P(('rep', 'exp')), may hold values from 0 to 15, all different within a row; in each aligned block of 128 rows (0 to 127, 128 to 255, ...) at most 72 rows name the same one
- route_weights: float32 [65536, 8], P(('rep', 'exp')), may hold values from 0.05 to 1
- placement_map: int32 [16], replicated, may hold values from 0 to 15, each once
- w_gate: bfloat16 [16, 2048, 384], P('exp', 'rep'), may hold values from -0.125 to 0.125
- w_up: bfloat16 [16, 2048, 384], P('exp', 'rep'), may hold values from -0.125 to 0.125
- down_rows: bfloat16 [16, 2048, 384], P('exp', 'rep'), may hold values from -0.3125 to 0.3125
Outputs:
- mixed: bfloat16 [65536, 2048], P(('rep', 'exp'))
Inputs may be any that keep to these rules, and one draw needn't show every extreme that they name: `expert_ids`: each row names 8 different experts. Within each device's aligned block of 128 rows no expert is named by more than 72 rows, a bound that some block reaches. `placement_map`: A permutation: every storage index is used once.
All inputs are finite; a program needn't handle non-finite values.
Results may differ from a plain program's by a relative error of at most 0.0057.
Values may be sent and summed in bfloat16 or wider, within the bound.
No kernel may reach another device: no remote copies, remote signals or barrier semaphores. Data moves between devices by JAX's collectives and lax.ppermute only.
A program may use at most 64 MiB of HBM per device.

v0:
```python
import jax
import jax.numpy as jnp
from jax import lax
from jax.sharding import PartitionSpec as P

CAP = 72


def apply_experts(received, weights):
    sources, local_count, capacity, model_width = received.shape
    row_block = received[:, 0].reshape(-1, model_width)
    gate_value = jnp.dot(row_block, weights[0, 0], preferred_element_type=jnp.float32)
    up_value = jnp.dot(row_block, weights[1, 0], preferred_element_type=jnp.float32)
    hidden = (jax.nn.silu(gate_value) * up_value).astype(jnp.bfloat16)
    result = lax.dot_general(
        hidden, weights[2, 0], (((1,), (1,)), ((), ())), preferred_element_type=jnp.float32
    )
    results = [result.astype(jnp.bfloat16).reshape(sources, capacity, model_width)]
    return jnp.stack(results, axis=1)


def on_device(tokens, expert_ids, route_weights, placement_map, w_gate, w_up, down_rows):
    tok_rows, top_count = expert_ids.shape
    experts = placement_map.shape[0]
    local_experts = w_gate.shape[0]
    model_width = tokens.shape[1]
    groups = lax.axis_size("exp")
    expert_range = jnp.arange(experts, dtype=jnp.int32)
    slot_ids = jnp.sum(jnp.where(expert_ids[:, :, None] == expert_range, placement_map, 0), axis=2)
    flat_slots = slot_ids.reshape(-1)
    onehot = (flat_slots[:, None] == expert_range).astype(jnp.int32)
    position = jnp.sum((jnp.cumsum(onehot, axis=0) - 1) * onehot, axis=1)
    target = flat_slots * CAP + position
    row_owner = jnp.arange(tok_rows * top_count, dtype=jnp.int32) // top_count
    source = jnp.full((experts * CAP,), tok_rows, jnp.int32).at[target].set(row_owner)
    outgoing = jnp.take(tokens, source, axis=0, mode="fill", fill_value=0)
    outgoing = outgoing.reshape(groups, local_experts, CAP, model_width)
    stacked = jnp.stack([w_gate, w_up, down_rows])
    stacked = lax.all_gather(stacked, "rep", axis=2, tiled=True)
    received = lax.all_to_all(outgoing, "exp", split_axis=0, concat_axis=0, tiled=True)
    returned = lax.all_to_all(
        apply_experts(received, stacked), "exp", split_axis=0, concat_axis=0, tiled=True
    )
    returned = returned.reshape(experts * CAP, model_width)
    picked = jnp.take(returned, target, axis=0).reshape(tok_rows, top_count, model_width)
    mixed = jnp.sum(route_weights[:, :, None] * picked.astype(jnp.float32), axis=1)
    return mixed.astype(jnp.bfloat16)


def solution(mesh):
    return jax.shard_map(
        on_device,
        mesh=mesh,
        in_specs=(
            P(("rep", "exp"), None),
            P(("rep", "exp"), None),
            P(("rep", "exp"), None),
            P(),
            P("exp", "rep", None),
            P("exp", "rep", None),
            P("exp", "rep", None),
        ),
        out_specs=P(("rep", "exp"), None),
        check_vma=False,
    )
```

profile of v0, /device:TPU:6, one launch (start us, length us, event | category | flops | bytes accessed | tf_op | source)
XLA Modules:
  0.0 294.3 jit_solution(9185044675160613837)
XLA Ops:
  6.5 0.0 copy-start
  6.5 0.0 all-gather.2.cloned.1.call-start
  6.5 1.6 pad_maximum_fusion
  8.1 0.0 all-gather.2.cloned.1.call-update
  8.1 0.8 select_reduce_fusion
  8.9 0.1 copy.23
  9.0 0.1 eq.42
  9.1 0.1 reshape.92
  9.3 4.5 %reduce-window.6 = s32[16,8,128]{2,1,0:T(8,128)S(1)} reduce-window(s32[16,8,128]{2,1,0:T(8,128)S(1)} %fusion.5, s32[]{:T(128)} %constant.51.clone.1), window={size=1x1x128 pad=0_0x0_0x127_0}, to_apply=%region_1.2 | reduce-window | flops 2080768 | bytes 131076 | tf_op jit(solution)/shard_map/reduce-window
  13.8 0.1 slice.24
  13.9 0.1 copy.25
  14.0 0.1 copy.26
  14.1 0.1 add_add_fusion
  14.2 0.1 copy.29
  14.3 0.1 mul.41
  14.4 4.3 %scatter_custom_fusion = s32[1152]{0:T(1024)S(1)} fusion(s32[1024]{0:T(1024)S(1)} %bitcast.54, s32[1024]{0:T(1024)S(1)} %add_select_fusion, s32[]{:T(128)} %constant.56.clone.1), kind=kCustom, calls=%fused_computation.35 | custom fusion | bytes 4612 | tf_op jit(solution)/shard_map/scatter | solution.py:35
  18.8 0.1 broadcast_in_dim.44
  18.9 0.0 copy-done
  18.9 6.0 %gather_fusion = bf16[1152,2048]{1,0:T(8,128)(2,1)} fusion(bf16[128,2048]{1,0:T(8,128)(2,1)S(1)} %copy-done, s32[2048]{0:T(1024)S(1)} %pad_clamp_fusion), kind=kCustom, calls=%fused_computation | custom fusion | bytes 9441792 | tf_op jit(solution)/shard_map/jit(_take)/gather | solution.py:36
  24.9 2.7 broadcast_select_fusion
  27.7 116.0 %all_to_all.10 = bf16[16,1,72,2048]{3,2,1,0:T(8,128)(2,1)} all-to-all(bf16[16,1,72,2048]{3,2,1,0:T(8,128)(2,1)S(1)} %broadcast_select_fusion), channel_id=1, replica_groups=mesh['rep'=32,'exp'=16] {'exp'}, dimensions={0} | all-to-all | bytes 9437184 | tf_op jit(solution)/shard_map/all_to_all | solution.py:40
  143.6 0.0 all-gather.2.cloned.1.call-done
  143.6 4.9 %fusion.1 = f32[1152,384]{1,0:T(8,128)S(1)} fusion(bf16[1152,2048]{1,0:T(8,128)(2,1)} %bitcast.46, bf16[3,1,2048,384]{3,2,1,0:T(8,128)(2,1)} %all-gather.2.cloned.1.call-done), kind=kOutput, calls=%fused_computation.12 | convolution fusion | flops 1811939328 | bytes 8060928 | tf_op jit(solution)/shard_map/dot_general | solution.py:12
  148.6 9.4 %convolution_convert_fusion = bf16[1152,2048]{1,0:T(8,128)(2,1)} fusion(bf16[3,1,2048,384]{3,2,1,0:T(8,128)(2,1)} %all-gather.2.cloned.1.call-done, bf16[1152,2048]{1,0:T(8,128)(2,1)} %bitcast.47, f32[1152,384]{1,0:T(8,128)S(1)} %fusion.1), kind=kOutput, calls=%fused_computation.4 | convolution fusion | flops 3628892160 | bytes 14352384 | tf_op jit(solution)/shard_map/dot_general | solution.py:15
  157.9 4.7 %all-to-all-start.1 = ((bf16[16,1,72,2048]{3,2,1,0:T(8,128)(2,1)}), bf16[16,1,72,2048]{3,2,1,0:T(8,128)(2,1)}, u32[]{:S(2)}, u32[]{:S(2)}) async-start(bf16[16,1,72,2048]{3,2,1,0:T(8,128)(2,1)} %bitcast.45), calls=%async_computation.1 | async-start | bytes 9437184 | tf_op jit(solution)/shard_map/all_to_all | solution.py:41
  162.6 0.1 reduce_sum.33
  162.8 0.1 copy.28
  162.9 0.0 copy-done.1
  162.9 0.1 copy.22
  163.0 106.3 %all-to-all-done.1 = bf16[16,1,72,2048]{3,2,1,0:T(8,128)(2,1)} async-done(((bf16[16,1,72,2048]{3,2,1,0:T(8,128)(2,1)}), bf16[16,1,72,2048]{3,2,1,0:T(8,128)(2,1)}, u32[]{:S(2)}, u32[]{:S(2)}) %all-to-all-start.1) | async-done | bytes 4718624 | tf_op jit(solution)/shard_map/all_to_all | solution.py:41
  269.4 11.8 %gather_fusion.1 = bf16[1024,2048]{1,0:T(8,128)(2,1)} fusion(bf16[1152,2048]{1,0:T(8,128)(2,1)} %bitcast.15, s32[1024]{0:T(1024)S(1)} %broadcast_clamp_fusion), kind=kCustom, calls=%fused_computation.1 | custom fusion | bytes 8392704 | tf_op jit(solution)/shard_map/jit(_take)/gather | solution.py:45
  281.2 6.3 %multiply_reduce_fusion = bf16[128,2048]{1,0:T(8,128)(2,1)} fusion(bf16[1024,2048]{1,0:T(8,128)(2,1)} %gather_fusion.1, f32[128,8]{1,0:T(8,128)S(1)} %copy.22, pred[128,8]{1,0:T(8,128)(4,1)S(1)} %copy.28), kind=kLoop, calls=%fused_computation.3 | loop fusion | flops 8126464 | bytes 4723712 | tf_op jit(solution)/shard_map/reduce_sum | solution.py:46
  (14 shorter events, 0.2 us)
Async XLA Ops:
  6.5 12.4 %copy-start = (bf16[128,2048]{1,0:T(8,128)(2,1)S(1)}, bf16[128,2048]{1,0:T(8,128)(2,1)}, u32[]{:S(2)}) copy-start(bf16[128,2048]{1,0:T(8,128)(2,1)} %param.7) | copy-start | bytes 1572868
  6.5 137.1 %all-gather.2.cloned.1.call-start = ((), (), s32[]{:S(2)}) async-start(), calls=%async_computation.2 | async-start | bytes 4866048 | tf_op jit(solution)/shard_map/all_gather | solution.py:39
  157.9 5.0 %copy-start.1 = (f32[128,8]{0,1:T(8,128)S(1)}, f32[128,8]{0,1:T(8,128)}, u32[]{:S(2)}) copy-start(f32[128,8]{0,1:T(8,128)} %param.9) | copy-start | bytes 12292
  157.9 111.5 %all-to-all-start.1 = ((bf16[16,1,72,2048]{3,2,1,0:T(8,128)(2,1)}), bf16[16,1,72,2048]{3,2,1,0:T(8,128)(2,1)}, u32[]{:S(2)}, u32[]{:S(2)}) async-start(bf16[16,1,72,2048]{3,2,1,0:T(8,128)(2,1)} %bitcast.45), calls=%async_computation.1 | async-start | bytes 9437184 | tf_op jit(solution)/shard_map/all_to_all | solution.py:41
Sparse Core Ops, SparseCore 0:
  10.5 89.6 all-gather.1
where the time goes:
time: 295 us; the launch traced here: 294 us
  blocking collectives  116 us (39%)
  waiting for transfers between devices  106 us (36%)
  local copies, waits for them, and re-layouts  23.4 us (8%)
  other arithmetic  16.1 us (5%)
  matrix products  14.3 us (5%)
  between operations  13.5 us (5%)
  starting transfers between devices  4.69 us (2%)
    all_to_all x1, blocking collectives, on_device(): lax.all_to_all(outgoing, 'exp', split_axis=0, concat_axis=0, tiled=True)  116 us
    all_to_all x1, waiting for transfers between devices, on_device(): lax.all_to_all(apply_experts(received, stacked), 'exp', split_axis=0, con...  106 us
    gather x1, local copies, waits for them, and re-layouts, on_device(): jnp.take(returned, target, axis=0).reshape(tok_rows, top_count, model_width)  11.8 us
    dot_general x1, matrix products, apply_experts(): lax.dot_general(hidden, weights[2, 0], (((1,), (1,)), ((), ())), preferre...  9.35 us
    reduce_sum x1, other arithmetic, on_device(): jnp.sum(route_weights[:, :, None] * picked.astype(jnp.float32), axis=1)  6.27 us
    gather x1, local copies, waits for them, and re-layouts, on_device(): outgoing = jnp.take(tokens, source, axis=0, mode='fill', fill_value=0)  6.02 us
  transfers between devices with their start and end apart: 2, of which 1 were waited for; matrix products, arithmetic and copies ran while one was open for 7% of the time, Pallas kernels for 0%

commit v1 on v0

--- a/solution.py
+++ b/solution.py
@@ -25,15 +25,22 @@
     local_experts = w_gate.shape[0]
     model_width = tokens.shape[1]
     groups = lax.axis_size("exp")
+    slots_total = experts * CAP
     expert_range = jnp.arange(experts, dtype=jnp.int32)
     slot_ids = jnp.sum(jnp.where(expert_ids[:, :, None] == expert_range, placement_map, 0), axis=2)
-    flat_slots = slot_ids.reshape(-1)
-    onehot = (flat_slots[:, None] == expert_range).astype(jnp.int32)
-    position = jnp.sum((jnp.cumsum(onehot, axis=0) - 1) * onehot, axis=1)
-    target = flat_slots * CAP + position
-    row_owner = jnp.arange(tok_rows * top_count, dtype=jnp.int32) // top_count
-    source = jnp.full((experts * CAP,), tok_rows, jnp.int32).at[target].set(row_owner)
-    outgoing = jnp.take(tokens, source, axis=0, mode="fill", fill_value=0)
+    slot_hot = slot_ids[:, :, None] == expert_range
+    token_hot = jnp.sum(slot_hot.astype(jnp.float32), axis=1).astype(jnp.bfloat16)
+    row_range = jnp.arange(tok_rows, dtype=jnp.int32)
+    earlier = (row_range[None, :] < row_range[:, None]).astype(jnp.bfloat16)
+    before = jnp.dot(earlier, token_hot, preferred_element_type=jnp.float32)
+    position = jnp.sum(jnp.where(slot_hot, before[:, None, :], 0.0), axis=2).astype(jnp.int32)
+    target = slot_ids * CAP + position
+    slot_range = jnp.arange(slots_total, dtype=jnp.int32)
+    hits = target[:, :, None] == slot_range
+    scatter = jnp.sum(hits.astype(jnp.float32), axis=1).astype(jnp.bfloat16)
+    outgoing = lax.dot_general(
+        scatter, tokens, (((0,), (0,)), ((), ())), preferred_element_type=jnp.float32
+    ).astype(jnp.bfloat16)
     outgoing = outgoing.reshape(groups, local_experts, CAP, model_width)
     stacked = jnp.stack([w_gate, w_up, down_rows])
     stacked = lax.all_gather(stacked, "rep", axis=2, tiled=True)
@@ -41,9 +48,12 @@
     returned = lax.all_to_all(
         apply_experts(received, stacked), "exp", split_axis=0, concat_axis=0, tiled=True
     )
-    returned = returned.reshape(experts * CAP, model_width)
-    picked = jnp.take(returned, target, axis=0).reshape(tok_rows, top_count, model_width)
-    mixed = jnp.sum(route_weights[:, :, None] * picked.astype(jnp.float32), axis=1)
+    returned = returned.reshape(slots_total, model_width)
+    combine = jnp.sum(jnp.where(hits, route_weights[:, :, None], 0.0), axis=1)
+    combine_hi = combine.astype(jnp.bfloat16)
+    combine_lo = (combine - combine_hi.astype(jnp.float32)).astype(jnp.bfloat16)
+    mixed = jnp.dot(combine_hi, returned, preferred_element_type=jnp.float32)
+    mixed = mixed + jnp.dot(combine_lo, returned, preferred_element_type=jnp.float32)
     return mixed.astype(jnp.bfloat16)
 
 

time: 295 us -> 265 us (0.90)
  blocking collectives: 116 us -> 226 us
  waiting for transfers between devices: 106 us -> 0.02 us
  local copies, waits for them, and re-layouts: 23.4 us -> 0.89 us
  other arithmetic: 16.1 us -> 5.27 us
  starting transfers between devices: 4.69 us -> 0.01 us
  matrix products: 14.3 us -> 18.4 us
    all_to_all x0 -> x1, blocking collectives: none -> 110 us  [on_device(): lax.all_to_all(apply_experts(received, stacked), 'exp', split_axis=0, con...]
    all_to_all x1 -> x0, waiting for transfers between devices: 106 us -> none  [on_device(): lax.all_to_all(apply_experts(received, stacked), 'exp', split_axis=0, con...]
    gather x2 -> x0, local copies, waits for them, and re-layouts: 17.8 us -> none  [the longest x1 11.8 us: on_device(): jnp.take(returned, target, axis=0).reshape(tok_rows, top_count, model_width)]
    all_to_all x1 -> x0, starting transfers between devices: 4.69 us -> none  [on_device(): lax.all_to_all(apply_experts(received, stacked), 'exp', split_axis=0, con...]
    another operation x2 -> x0, other arithmetic: 4.55 us -> none
    scatter x1 -> x0, local copies, waits for them, and re-layouts: 4.32 us -> none  [on_device(): jnp.full((experts * CAP,), tok_rows, jnp.int32).at[target].set(row_owner)]
    dot_general x0 -> x4, matrix products: none -> 4.12 us  [the longest x1 1.7 us: on_device(): jnp.dot(combine_lo, returned, preferred_element_type=jnp.float32)]
    reduce_sum x2 -> x3, other arithmetic: 6.3 us -> 2.89 us  [the longest x1 2.84 us: on_device(): combine = jnp.sum(jnp.where(hits, route_weights[:, :, None], 0.0), axis=1)]
  transfers between devices with their start and end apart: 2 -> 1, of which waited for: 1 -> 0; matrix products, arithmetic and copies ran while one was open for 7% -> 2% of each run, Pallas kernels for 0% -> 0%
where the time goes in v1:
time: 265 us; the launch traced here: 264 us
  blocking collectives  226 us (85%)
  matrix products  18.4 us (7%)
  between operations  13.5 us (5%)
  other arithmetic  5.27 us (2%)
    all_to_all x1, blocking collectives, on_device(): lax.all_to_all(outgoing, 'exp', split_axis=0, concat_axis=0, tiled=True)  116 us
    all_to_all x1, blocking collectives, on_device(): lax.all_to_all(apply_experts(received, stacked), 'exp', split_axis=0, con...  110 us
    dot_general x1, matrix products, apply_experts(): lax.dot_general(hidden, weights[2, 0], (((1,), (1,)), ((), ())), preferre...  9.35 us
  transfers between devices with their start and end apart: 1, of which 0 were waited for; matrix products, arithmetic and copies ran while one was open for 2% of the time, Pallas kernels for 0%

profile of v1, /device:TPU:6, one launch (start us, length us, event | category | flops | bytes accessed | tf_op | source)
XLA Modules:
  0.0 264.3 jit_solution(10686982494979855700)
XLA Ops:
  6.5 0.0 copy-start
  6.5 0.0 all-gather.2.cloned.1.call-start
  6.5 1.6 pad_maximum_fusion
  8.1 0.0 all-gather.2.cloned.1.call-update
  8.1 0.8 select_reduce_fusion.2
  9.0 0.1 fusion.8
  9.2 0.1 copy.16
  9.3 0.8 copy.17
  10.0 2.8 %select_reduce_fusion = (f32[128,1152]{1,0:T(8,128)S(1)}, bf16[128,1152]{1,0:T(8,128)(2,1)S(1)}) fusion(f32[128,8]{1,0:T(8,128)S(1)} %copy.17, s32[128,8]{1,0:T(8,128)S(1)} %copy.16), kind=kLoop, calls=%fused_computation.3 | loop fusion | flops 5603328 | bytes 892928 | tf_op jit(solution)/shard_map/reduce_sum | solution.py:52
  12.9 0.0 copy-done
  12.9 1.4 convolution_convert_fusion.1
  14.3 116.0 %all_to_all.10 = bf16[16,1,72,2048]{3,2,1,0:T(8,128)(2,1)} all-to-all(bf16[16,1,72,2048]{3,2,1,0:T(8,128)(2,1)S(1)} %bitcast.31), channel_id=1, replica_groups=mesh['rep'=32,'exp'=16] {'exp'}, dimensions={0} | all-to-all | bytes 9437184 | tf_op jit(solution)/shard_map/all_to_all | solution.py:47
  130.3 0.0 all-gather.2.cloned.1.call-done
  130.3 4.9 %fusion.2 = f32[1152,384]{1,0:T(8,128)S(1)} fusion(bf16[1152,2048]{1,0:T(8,128)(2,1)} %bitcast.32, bf16[3,1,2048,384]{3,2,1,0:T(8,128)(2,1)} %all-gather.2.cloned.1.call-done), kind=kOutput, calls=%fused_computation.12 | convolution fusion | flops 1811939328 | bytes 8060928 | tf_op jit(solution)/shard_map/dot_general | solution.py:12
  135.2 9.4 %convolution_convert_fusion = bf16[1152,2048]{1,0:T(8,128)(2,1)} fusion(bf16[3,1,2048,384]{3,2,1,0:T(8,128)(2,1)} %all-gather.2.cloned.1.call-done, bf16[1152,2048]{1,0:T(8,128)(2,1)} %bitcast.33, f32[1152,384]{1,0:T(8,128)S(1)} %fusion.2), kind=kOutput, calls=%fused_computation | convolution fusion | flops 3628892160 | bytes 14352384 | tf_op jit(solution)/shard_map/dot_general | solution.py:15
  144.5 110.4 %all_to_all.11 = bf16[16,1,72,2048]{3,2,1,0:T(8,128)(2,1)S(1)} all-to-all(bf16[16,1,72,2048]{3,2,1,0:T(8,128)(2,1)} %bitcast.34), channel_id=1, replica_groups=mesh['rep'=32,'exp'=16] {'exp'}, dimensions={0} | all-to-all | bytes 9437184 | tf_op jit(solution)/shard_map/all_to_all | solution.py:48
  254.9 0.9 fusion.6
  255.8 1.7 fusion.1
  (3 shorter events, 0.1 us)
Async XLA Ops:
  6.5 6.4 %copy-start = (bf16[128,2048]{1,0:T(8,128)(2,1)S(1)}, bf16[128,2048]{1,0:T(8,128)(2,1)}, u32[]{:S(2)}) copy-start(bf16[128,2048]{1,0:T(8,128)(2,1)} %param.7) | copy-start | bytes 1572868
  6.5 123.7 %all-gather.2.cloned.1.call-start = ((), (), s32[]{:S(2)}) async-start(), calls=%async_computation.2 | async-start | bytes 4866048 | tf_op jit(solution)/shard_map/all_gather | solution.py:46
Sparse Core Ops, SparseCore 0:
  10.5 93.7 all-gather.1

commit v2 on v1

--- a/solution.py
+++ b/solution.py
@@ -1,7 +1,7 @@
 import jax
 import jax.numpy as jnp
 from jax import lax
-from jax.sharding import PartitionSpec as P
+from jax.sharding import Mesh, PartitionSpec as P
 
 CAP = 72
 
@@ -24,7 +24,7 @@
     experts = placement_map.shape[0]
     local_experts = w_gate.shape[0]
     model_width = tokens.shape[1]
-    groups = lax.axis_size("exp")
+    groups = experts
     slots_total = experts * CAP
     expert_range = jnp.arange(experts, dtype=jnp.int32)
     slot_ids = jnp.sum(jnp.where(expert_ids[:, :, None] == expert_range, placement_map, 0), axis=2)
@@ -43,10 +43,14 @@
     ).astype(jnp.bfloat16)
     outgoing = outgoing.reshape(groups, local_experts, CAP, model_width)
     stacked = jnp.stack([w_gate, w_up, down_rows])
-    stacked = lax.all_gather(stacked, "rep", axis=2, tiled=True)
-    received = lax.all_to_all(outgoing, "exp", split_axis=0, concat_axis=0, tiled=True)
+    stacked = lax.all_gather(stacked, "y", axis=1, tiled=True)
+    stacked = lax.all_to_all(stacked, ("x", "c"), split_axis=1, concat_axis=1, tiled=True)
+    stacked = stacked.reshape(3, 1, -1, stacked.shape[-1])
+    stacked = lax.all_gather(stacked, "zh", axis=2, tiled=True)
+    team = ("x", "c", "zl")
+    received = lax.all_to_all(outgoing, team, split_axis=0, concat_axis=0, tiled=True)
     returned = lax.all_to_all(
-        apply_experts(received, stacked), "exp", split_axis=0, concat_axis=0, tiled=True
+        apply_experts(received, stacked), team, split_axis=0, concat_axis=0, tiled=True
     )
     returned = returned.reshape(slots_total, model_width)
     combine = jnp.sum(jnp.where(hits, route_weights[:, :, None], 0.0), axis=1)
@@ -58,18 +62,21 @@
 
 
 def solution(mesh):
+    fine = Mesh(mesh.devices.reshape(4, 4, 2, 8, 2), ("zh", "x", "c", "y", "zl"))
+    rows = ("zh", "x", "c", "y", "zl")
+    weight_spec = P(("y", "zl"), ("zh", "x", "c"), None)
     return jax.shard_map(
         on_device,
-        mesh=mesh,
+        mesh=fine,
         in_specs=(
-            P(("rep", "exp"), None),
-            P(("rep", "exp"), None),
-            P(("rep", "exp"), None),
+            P(rows, None),
+            P(rows, None),
+            P(rows, None),
             P(),
-            P("exp", "rep", None),
-            P("exp", "rep", None),
-            P("exp", "rep", None),
+            weight_spec,
+            weight_spec,
+            weight_spec,
         ),
-        out_specs=P(("rep", "exp"), None),
+        out_specs=P(rows, None),
         check_vma=False,
     )

time: 265 us -> 299 us (1.13)
  waiting for transfers between devices: 0.02 us -> 186 us
  blocking collectives: 226 us -> 58.3 us
  starting transfers between devices: 0.01 us -> 11.3 us
    all_to_all x2 -> x1, blocking collectives: 226 us -> 58.3 us  [on_device(): lax.all_to_all(apply_experts(received, stacked), team, split_axis=0, conc...]
    all_to_all x0 -> x2, waiting for transfers between devices: none -> 130 us  [the longest x1 122 us: on_device(): lax.all_to_all(outgoing, team, split_axis=0, concat_axis=0, tiled=True)]
    all_gather x1 -> x2, waiting for transfers between devices: 0.01 us -> 55.4 us  [the longest x1 46.5 us: on_device(): stacked = lax.all_gather(stacked, 'y', axis=1, tiled=True)]
    all_to_all x0 -> x2, starting transfers between devices: none -> 11.2 us  [the longest x1 6.43 us: on_device(): lax.all_to_all(outgoing, team, split_axis=0, concat_axis=0, tiled=True)]
  transfers between devices with their start and end apart: 1 -> 4, of which waited for: 0 -> 4; matrix products, arithmetic and copies ran while one was open for 2% -> 3% of each run, Pallas kernels for 0% -> 0%
where the time goes in v2:
time: 299 us; the launch traced here: 297 us
  waiting for transfers between devices  186 us (62%)
  blocking collectives  58.3 us (19%)
  matrix products  20.6 us (7%)
  between operations  13.5 us (5%)
  starting transfers between devices  11.3 us (4%)
  other arithmetic  5.27 us (2%)
    all_to_all x1, waiting for transfers between devices, on_device(): lax.all_to_all(outgoing, team, split_axis=0, concat_axis=0, tiled=True)  122 us
    all_to_all x1, blocking collectives, on_device(): lax.all_to_all(apply_experts(received, stacked), team, split_axis=0, conc...  58.3 us
    all_gather x1, waiting for transfers between devices, on_device(): stacked = lax.all_gather(stacked, 'y', axis=1, tiled=True)  46.5 us
    dot_general x1, matrix products, apply_experts(): lax.dot_general(hidden, weights[2, 0], (((1,), (1,)), ((), ())), preferre...  9.35 us
    all_gather x1, waiting for transfers between devices, on_device(): stacked = lax.all_gather(stacked, 'zh', axis=2, tiled=True)  8.98 us
    all_to_all x1, waiting for transfers between devices, on_device(): lax.all_to_all(stacked, ('x', 'c'), split_axis=1, concat_axis=1, tiled=True)  7.71 us
    all_to_all x1, starting transfers between devices, on_device(): lax.all_to_all(outgoing, team, split_axis=0, concat_axis=0, tiled=True)  6.43 us
  transfers between devices with their start and end apart: 4, of which 4 were waited for; matrix products, arithmetic and copies ran while one was open for 3% of the time, Pallas kernels for 0%

profile of v2, /device:TPU:6, one launch (start us, length us, event | category | flops | bytes accessed | tf_op | source)
XLA Modules:
  0.0 296.7 jit_solution(1834866640219646108)
XLA Ops:
  6.5 0.0 copy-start
  6.5 0.0 all-gather.3.cloned.1.call-start
  6.5 1.6 pad_maximum_fusion
  8.1 0.0 all-gather.3.cloned.1.call-update
  8.1 0.8 select_reduce_fusion.2
  9.0 46.5 %all-gather.3.cloned.1.call-done = bf16[3,8,64,384]{3,2,0,1:T(8,128)(2,1)} async-done(((bf16[3,1,64,384]{3,2,0,1:T(8,128)(2,1)}), bf16[3,8,64,384]{3,2,0,1:T(8,128)(2,1)}) %all-gather.3.cloned.1.call-update) | async-done | bytes 1179664 | tf_op jit(solution)/shard_map/all_gather | solution.py:46
  55.4 4.8 %all-to-all-start.1 = ((bf16[3,8,64,384]{3,2,0,1:T(8,128)(2,1)}), bf16[3,8,64,384]{3,2,0,1:T(8,128)(2,1)S(1)}, u32[]{:S(2)}, u32[]{:S(2)}) async-start(bf16[3,8,64,384]{3,2,0,1:T(8,128)(2,1)} %all-gather.3.cloned.1.call-done), calls=%async_computation.1 | async-start | bytes 2359296 | tf_op jit(solution)/shard_map/all_to_all | solution.py:47
  60.2 0.1 fusion.8
  60.4 0.1 copy.28
  60.5 0.8 copy.29
  61.3 2.8 select_reduce_fusion
  64.1 0.0 copy-done
  64.2 3.6 %convolution_convert_fusion.1 = bf16[1152,2048]{1,0:T(8,128)(2,1)} fusion(bf16[128,2048]{1,0:T(8,128)(2,1)S(1)} %copy-done, bf16[128,1152]{1,0:T(8,128)(2,1)S(1)} %get-tuple-element.6), kind=kOutput, calls=%fused_computation.1 | convolution fusion | flops 606339072 | bytes 5537792 | tf_op jit(solution)/shard_map/dot_general | solution.py:41
  67.8 7.7 %all-to-all-done.1 = bf16[3,8,64,384]{3,2,0,1:T(8,128)(2,1)S(1)} async-done(((bf16[3,8,64,384]{3,2,0,1:T(8,128)(2,1)}), bf16[3,8,64,384]{3,2,0,1:T(8,128)(2,1)S(1)}, u32[]{:S(2)}, u32[]{:S(2)}) %all-to-all-start.1) | async-done | bytes 1179680 | tf_op jit(solution)/shard_map/all_to_all | solution.py:47
  75.5 6.4 %all-to-all-start = ((bf16[16,1,72,2048]{3,2,1,0:T(8,128)(2,1)}), bf16[16,1,72,2048]{3,2,1,0:T(8,128)(2,1)}, u32[]{:S(2)}, u32[]{:S(2)}) async-start(bf16[16,1,72,2048]{3,2,1,0:T(8,128)(2,1)} %bitcast.32), calls=%async_computation | async-start | bytes 9437184 | tf_op jit(solution)/shard_map/all_to_all | solution.py:51
  82.0 0.0 all-gather.5.cloned.1.call-start
  82.0 1.2 copy.31
  83.2 0.0 all-gather.5.cloned.1.call-update
  83.2 122.5 %all-to-all-done = bf16[16,1,72,2048]{3,2,1,0:T(8,128)(2,1)} async-done(((bf16[16,1,72,2048]{3,2,1,0:T(8,128)(2,1)}), bf16[16,1,72,2048]{3,2,1,0:T(8,128)(2,1)}, u32[]{:S(2)}, u32[]{:S(2)}) %all-to-all-start) | async-done | bytes 4718624 | tf_op jit(solution)/shard_map/all_to_all | solution.py:51
  205.7 9.0 %all-gather.5.cloned.1.call-done = bf16[3,1,2048,384]{3,2,0,1:T(8,128)(2,1)} async-done(((bf16[3,1,512,384]{3,2,0,1:T(8,128)(2,1)}), bf16[3,1,2048,384]{3,2,0,1:T(8,128)(2,1)}) %all-gather.5.cloned.1.call-update) | async-done | bytes 4718608 | tf_op jit(solution)/shard_map/all_gather | solution.py:49
  214.7 4.9 %fusion.2 = f32[1152,384]{1,0:T(8,128)S(1)} fusion(bf16[1152,2048]{1,0:T(8,128)(2,1)} %bitcast.2, bf16[3,1,2048,384]{3,2,0,1:T(8,128)(2,1)} %all-gather.5.cloned.1.call-done), kind=kOutput, calls=%fused_computation.12 | convolution fusion | flops 1811939328 | bytes 8060928 | tf_op jit(solution)/shard_map/dot_general | solution.py:12
  219.6 9.4 %convolution_convert_fusion = bf16[1152,2048]{1,0:T(8,128)(2,1)} fusion(bf16[3,1,2048,384]{3,2,0,1:T(8,128)(2,1)} %all-gather.5.cloned.1.call-done, bf16[1152,2048]{1,0:T(8,128)(2,1)} %bitcast.2, f32[1152,384]{1,0:T(8,128)S(1)} %fusion.2), kind=kOutput, calls=%fused_computation | convolution fusion | flops 3628892160 | bytes 14352384 | tf_op jit(solution)/shard_map/dot_general | solution.py:15
  228.9 58.3 %all_to_all.15 = bf16[16,1,72,2048]{3,2,1,0:T(8,128)(2,1)S(1)} all-to-all(bf16[16,1,72,2048]{3,2,1,0:T(8,128)(2,1)} %bitcast.33), channel_id=1, replica_groups=mesh['zh'=4,'x'=4,'c'=2,'y'=8,'zl'=2] {'x','c','zl'}, dimensions={0} | all-to-all | bytes 9437184 | tf_op jit(solution)/shard_map/all_to_all | solution.py:52
  287.3 0.9 fusion.6
  288.1 1.7 fusion.1
  (3 shorter events, 0.1 us)
Async XLA Ops:
  6.5 57.6 %copy-start = (bf16[128,2048]{1,0:T(8,128)(2,1)S(1)}, bf16[128,2048]{1,0:T(8,128)(2,1)}, u32[]{:S(2)}) copy-start(bf16[128,2048]{1,0:T(8,128)(2,1)} %param.7) | copy-start | bytes 1572868
  6.5 48.9 %all-gather.3.cloned.1.call-start = ((), (), s32[]{:S(2)}) async-start(), calls=%async_computation.3 | async-start | bytes 1327104 | tf_op jit(solution)/shard_map/all_gather | solution.py:46
  55.4 20.1 %all-to-all-start.1 = ((bf16[3,8,64,384]{3,2,0,1:T(8,128)(2,1)}), bf16[3,8,64,384]{3,2,0,1:T(8,128)(2,1)S(1)}, u32[]{:S(2)}, u32[]{:S(2)}) async-start(bf16[3,8,64,384]{3,2,0,1:T(8,128)(2,1)} %all-gather.3.cloned.1.call-done), calls=%async_computation.1 | async-start | bytes 2359296 | tf_op jit(solution)/shard_map/all_to_all | solution.py:47
  75.5 130.2 %all-to-all-start = ((bf16[16,1,72,2048]{3,2,1,0:T(8,128)(2,1)}), bf16[16,1,72,2048]{3,2,1,0:T(8,128)(2,1)}, u32[]{:S(2)}, u32[]{:S(2)}) async-start(bf16[16,1,72,2048]{3,2,1,0:T(8,128)(2,1)} %bitcast.32), calls=%async_computation | async-start | bytes 9437184 | tf_op jit(solution)/shard_map/all_to_all | solution.py:51
  82.0 132.7 %all-gather.5.cloned.1.call-start = ((), (), s32[]{:S(2)}) async-start(), calls=%async_computation.4 | async-start | bytes 5898240 | tf_op jit(solution)/shard_map/all_gather | solution.py:49
Sparse Core Ops, SparseCore 0:
  9.4 45.9 all-gather.2
  84.9 129.7 all-gather.4

commit v3 on v1

v3 whole, which is shorter than its diff:
```python
import jax
import jax.numpy as jnp
from jax import lax
from jax.sharding import PartitionSpec as P

CAP = 72


def apply_experts(received, weights):
    sources, local_count, capacity, model_width = received.shape
    row_block = received[:, 0].reshape(-1, model_width)
    gate_value = jnp.dot(row_block, weights[0][0], preferred_element_type=jnp.float32)
    up_value = jnp.dot(row_block, weights[1][0], preferred_element_type=jnp.float32)
    hidden = (jax.nn.silu(gate_value) * up_value).astype(jnp.bfloat16)
    result = lax.dot_general(
        hidden, weights[2][0], (((1,), (1,)), ((), ())), preferred_element_type=jnp.float32
    )
    results = [result.astype(jnp.bfloat16).reshape(sources, capacity, model_width)]
    return jnp.stack(results, axis=1)


def on_device(tokens, expert_ids, route_weights, placement_map, w_gate, w_up, down_rows):
    tok_rows, top_count = expert_ids.shape
    experts = placement_map.shape[0]
    local_experts = w_gate.shape[0]
    model_width = tokens.shape[1]
    groups = lax.axis_size("exp")
    slots_total = experts * CAP
    expert_range = jnp.arange(experts, dtype=jnp.int32)
    slot_ids = jnp.sum(jnp.where(expert_ids[:, :, None] == expert_range, placement_map, 0), axis=2)
    slot_hot = slot_ids[:, :, None] == expert_range
    token_hot = jnp.sum(slot_hot.astype(jnp.float32), axis=1)
    row_range = jnp.arange(tok_rows, dtype=jnp.int32)
    earlier = (row_range[None, :] < row_range[:, None]).astype(jnp.bfloat16)
    before = jnp.dot(earlier, token_hot.astype(jnp.bfloat16), preferred_element_type=jnp.float32)
    picked_weight = jnp.sum(jnp.where(slot_hot, route_weights[:, :, None], 0.0), axis=1)
    cap_range = jnp.arange(CAP, dtype=jnp.float32)
    placed = (before[:, :, None] == cap_range) & (token_hot[:, :, None] > 0.5)
    scatter = placed.astype(jnp.bfloat16).reshape(tok_rows, slots_total)
    outgoing = lax.dot_general(
        scatter, tokens, (((0,), (0,)), ((), ())), preferred_element_type=jnp.float32
    ).astype(jnp.bfloat16)
    outgoing = outgoing.reshape(groups, local_experts, CAP, model_width)
    gathered = [lax.all_gather(w, "rep", axis=1, tiled=True) for w in (w_gate, w_up, down_rows)]
    received = lax.all_to_all(outgoing, "exp", split_axis=0, concat_axis=0, tiled=True)
    returned = lax.all_to_all(
        apply_experts(received, gathered), "exp", split_axis=0, concat_axis=0, tiled=True
    )
    returned = returned.reshape(slots_total, model_width)
    combine = jnp.where(placed, picked_weight[:, :, None], 0.0).reshape(tok_rows, slots_total)
    combine_hi = combine.astype(jnp.bfloat16)
    combine_lo = (combine - combine_hi.astype(jnp.float32)).astype(jnp.bfloat16)
    mixed = jnp.dot(combine_hi, returned, preferred_element_type=jnp.float32)
    mixed = mixed + jnp.dot(combine_lo, returned, preferred_element_type=jnp.float32)
    return mixed.astype(jnp.bfloat16)


def solution(mesh):
    return jax.shard_map(
        on_device,
        mesh=mesh,
        in_specs=(
            P(("rep", "exp"), None),
            P(("rep", "exp"), None),
            P(("rep", "exp"), None),
            P(),
            P("exp", "rep", None),
            P("exp", "rep", None),
            P("exp", "rep", None),
        ),
        out_specs=P(("rep", "exp"), None),
        check_vma=False,
    )
```

time: 265 us -> 385 us (1.45)
  waiting for transfers between devices: 0.02 us -> 326 us
  blocking collectives: 226 us -> 0 us
  starting transfers between devices: 0.01 us -> 16.2 us
  matrix products: 18.4 us -> 25.1 us
    all_to_all x2 -> x0, blocking collectives: 226 us -> none  [the longest x1 116 us: on_device(): lax.all_to_all(outgoing, 'exp', split_axis=0, concat_axis=0, tiled=True)]
    all_gather x1 -> x3, waiting for transfers between devices: 0.01 us -> 181 us  [on_device(): lax.all_gather(w, 'rep', axis=1, tiled=True)]
    all_to_all x0 -> x2, waiting for transfers between devices: none -> 144 us  [the longest x1 110 us: on_device(): lax.all_to_all(apply_experts(received, gathered), 'exp', split_axis=0, co...]
    all_to_all x0 -> x2, starting transfers between devices: none -> 16.1 us  [the longest x1 9.06 us: on_device(): lax.all_to_all(outgoing, 'exp', split_axis=0, concat_axis=0, tiled=True)]
  transfers between devices with their start and end apart: 1 -> 5, of which waited for: 0 -> 5; matrix products, arithmetic and copies ran while one was open for 2% -> 1% of each run, Pallas kernels for 0% -> 0%
where the time goes in v3:
time: 385 us; the launch traced here: 383 us
  waiting for transfers between devices  326 us (85%)
  matrix products  25.1 us (7%)
  starting transfers between devices  16.2 us (4%)
  between operations  13.2 us (3%)
    all_gather x3, waiting for transfers between devices, on_device(): lax.all_gather(w, 'rep', axis=1, tiled=True)  181 us
    all_to_all x1, waiting for transfers between devices, on_device(): lax.all_to_all(apply_experts(received, gathered), 'exp', split_axis=0, co...  110 us
    all_to_all x1, waiting for transfers between devices, on_device(): lax.all_to_all(outgoing, 'exp', split_axis=0, concat_axis=0, tiled=True)  34.1 us
    dot_general x1, matrix products, apply_experts(): lax.dot_general(hidden, weights[2][0], (((1,), (1,)), ((), ())), preferre...  9.34 us
    all_to_all x1, starting transfers between devices, on_device(): lax.all_to_all(outgoing, 'exp', split_axis=0, concat_axis=0, tiled=True)  9.06 us
  transfers between devices with their start and end apart: 5, of which 5 were waited for; matrix products, arithmetic and copies ran while one was open for 1% of the time, Pallas kernels for 0%

profile of v3, /device:TPU:6, one launch (start us, length us, event | category | flops | bytes accessed | tf_op | source)
XLA Modules:
  0.0 383.1 jit_solution(2529467783592259514)
XLA Ops:
  6.5 0.0 copy-start
  6.5 0.8 select_reduce_fusion.1
  7.4 0.7 convert_reduce_fusion
  8.1 0.1 fusion.11
  8.3 0.1 eq.76
  8.4 0.2 fusion.10
  8.6 0.0 copy-done
  8.6 3.5 convolution_convert_fusion.1
  12.1 9.1 %all-to-all-start = ((bf16[16,1,72,2048]{3,2,1,0:T(8,128)(2,1)}), bf16[16,1,72,2048]{3,2,1,0:T(8,128)(2,1)}, u32[]{:S(2)}, u32[]{:S(2)}) async-start(bf16[16,1,72,2048]{3,2,1,0:T(8,128)(2,1)} %bitcast.35), calls=%async_computation | async-start | bytes 9437184 | tf_op jit(solution)/shard_map/all_to_all | solution.py:45
  21.2 0.0 all-gather.4.cloned.1.call-start
  21.3 0.7 all-gather.4.cloned.1.call-update
  21.9 0.0 all-gather.6.cloned.1.call-start
  22.0 0.7 all-gather.6.cloned.1.call-update
  22.7 0.0 all-gather.8.cloned.1.call-start
  22.7 0.7 all-gather.8.cloned.1.call-update
  23.4 71.3 %all-gather.4.cloned.1.call-done = bf16[1,2048,384]{2,1,0:T(8,128)(2,1)} async-done(((bf16[1,64,384]{2,1,0:T(8,128)(2,1)}), bf16[1,2048,384]{2,1,0:T(8,128)(2,1)}) %all-gather.4.cloned.1.call-update) | async-done | bytes 1572880 | tf_op jit(solution)/shard_map/all_gather | solution.py:44
  94.7 34.1 %all-to-all-done = bf16[16,1,72,2048]{3,2,1,0:T(8,128)(2,1)} async-done(((bf16[16,1,72,2048]{3,2,1,0:T(8,128)(2,1)}), bf16[16,1,72,2048]{3,2,1,0:T(8,128)(2,1)}, u32[]{:S(2)}, u32[]{:S(2)}) %all-to-all-start) | async-done | bytes 4718624 | tf_op jit(solution)/shard_map/all_to_all | solution.py:45
  128.8 4.9 %fusion.4 = f32[1152,384]{1,0:T(8,128)S(1)} fusion(bf16[1152,2048]{1,0:T(8,128)(2,1)} %bitcast.5, bf16[1,2048,384]{2,1,0:T(8,128)(2,1)} %all-gather.4.cloned.1.call-done), kind=kOutput, calls=%fused_computation.8 | convolution fusion | flops 1811939328 | bytes 8060928 | tf_op jit(solution)/shard_map/dot_general | solution.py:12
  133.7 49.7 %all-gather.6.cloned.1.call-done = bf16[1,2048,384]{2,1,0:T(8,128)(2,1)} async-done(((bf16[1,64,384]{2,1,0:T(8,128)(2,1)}), bf16[1,2048,384]{2,1,0:T(8,128)(2,1)}) %all-gather.6.cloned.1.call-update) | async-done | bytes 1572880 | tf_op jit(solution)/shard_map/all_gather | solution.py:44
  183.4 59.6 %all-gather.8.cloned.1.call-done = bf16[1,2048,384]{2,1,0:T(8,128)(2,1)} async-done(((bf16[1,64,384]{2,1,0:T(8,128)(2,1)}), bf16[1,2048,384]{2,1,0:T(8,128)(2,1)}) %all-gather.8.cloned.1.call-update) | async-done | bytes 1572880 | tf_op jit(solution)/shard_map/all_gather | solution.py:44
  243.0 9.3 %convolution_convert_fusion = bf16[1152,2048]{1,0:T(8,128)(2,1)} fusion(bf16[1,2048,384]{2,1,0:T(8,128)(2,1)} %all-gather.8.cloned.1.call-done, bf16[1152,2048]{1,0:T(8,128)(2,1)} %bitcast.5, f32[1152,384]{1,0:T(8,128)S(1)} %fusion.4, bf16[1,2048,384]{2,1,0:T(8,128)(2,1)} %all-gather.6.cloned.1.call-done), kind=kOutput, calls=%fused_computation | convolution fusion | flops 3628892160 | bytes 14352384 | tf_op jit(solution)/shard_map/dot_general | solution.py:15
  252.3 7.1 %all-to-all-start.1 = ((bf16[16,1,72,2048]{3,2,1,0:T(8,128)(2,1)}), bf16[16,1,72,2048]{3,2,1,0:T(8,128)(2,1)}, u32[]{:S(2)}, u32[]{:S(2)}) async-start(bf16[16,1,72,2048]{3,2,1,0:T(8,128)(2,1)} %bitcast.36), calls=%async_computation.1 | async-start | bytes 9437184 | tf_op jit(solution)/shard_map/all_to_all | solution.py:46
  259.4 0.1 select_convert_fusion
  259.5 0.2 fusion.8
  259.7 109.6 %all-to-all-done.1 = bf16[16,1,72,2048]{3,2,1,0:T(8,128)(2,1)} async-done(((bf16[16,1,72,2048]{3,2,1,0:T(8,128)(2,1)}), bf16[16,1,72,2048]{3,2,1,0:T(8,128)(2,1)}, u32[]{:S(2)}, u32[]{:S(2)}) %all-to-all-start.1) | async-done | bytes 4718624 | tf_op jit(solution)/shard_map/all_to_all | solution.py:46
  369.4 3.2 fusion.14
  372.6 4.0 %fusion.1 = bf16[128,2048]{1,0:T(8,128)(2,1)} fusion(f32[128,2048]{1,0:T(8,128)S(1)} %fusion.14, bf16[128,1152]{0,1:T(8,128)(2,1)S(1)} %bitcast.37, bf16[1152,2048]{1,0:T(8,128)(2,1)} %bitcast.11), kind=kOutput, calls=%fused_computation.5 | convolution fusion | flops 604504064 | bytes 6586368 | tf_op jit(solution)/shard_map/dot_general | solution.py:54
  (2 shorter events, 0.0 us)
Async XLA Ops:
  6.5 2.1 copy-start
  12.1 116.6 %all-to-all-start = ((bf16[16,1,72,2048]{3,2,1,0:T(8,128)(2,1)}), bf16[16,1,72,2048]{3,2,1,0:T(8,128)(2,1)}, u32[]{:S(2)}, u32[]{:S(2)}) async-start(bf16[16,1,72,2048]{3,2,1,0:T(8,128)(2,1)} %bitcast.35), calls=%async_computation | async-start | bytes 9437184 | tf_op jit(solution)/shard_map/all_to_all | solution.py:45
  21.2 73.5 %all-gather.4.cloned.1.call-start = ((), (), s32[]{:S(2)}) async-start(), calls=%async_computation.2 | async-start | bytes 1622016 | tf_op jit(solution)/shard_map/all_gather | solution.py:44
  21.9 161.5 %all-gather.6.cloned.1.call-start = ((), (), s32[]{:S(2)}) async-start(), calls=%async_computation.3 | async-start | bytes 1622016 | tf_op jit(solution)/shard_map/all_gather | solution.py:44
  22.7 220.3 %all-gather.8.cloned.1.call-start = ((), (), s32[]{:S(2)}) async-start(), calls=%async_computation.4 | async-start | bytes 1622016 | tf_op jit(solution)/shard_map/all_gather | solution.py:44
  252.3 117.0 %all-to-all-start.1 = ((bf16[16,1,72,2048]{3,2,1,0:T(8,128)(2,1)}), bf16[16,1,72,2048]{3,2,1,0:T(8,128)(2,1)}, u32[]{:S(2)}, u32[]{:S(2)}) async-start(bf16[16,1,72,2048]{3,2,1,0:T(8,128)(2,1)} %bitcast.36), calls=%async_computation.1 | async-start | bytes 9437184 | tf_op jit(solution)/shard_map/all_to_all | solution.py:46
Sparse Core Ops, SparseCore 0:
  25.2 69.4 all-gather.3
  97.8 85.5 all-gather.5
  186.5 56.4 all-gather.7

commit v4 on v1

--- a/solution.py
+++ b/solution.py
@@ -8,10 +8,13 @@
 
 def apply_experts(received, weights):
     sources, local_count, capacity, model_width = received.shape
+    hidden_width = weights.shape[-1]
     row_block = received[:, 0].reshape(-1, model_width)
-    gate_value = jnp.dot(row_block, weights[0, 0], preferred_element_type=jnp.float32)
-    up_value = jnp.dot(row_block, weights[1, 0], preferred_element_type=jnp.float32)
+    gate_up = jnp.concatenate([weights[0, 0], weights[1, 0]], axis=1)
+    both = jnp.dot(row_block, gate_up, preferred_element_type=jnp.float32)
+    gate_value, up_value = both[:, :hidden_width], both[:, hidden_width:]
     hidden = (jax.nn.silu(gate_value) * up_value).astype(jnp.bfloat16)
+    hidden = lax.optimization_barrier(hidden)
     result = lax.dot_general(
         hidden, weights[2, 0], (((1,), (1,)), ((), ())), preferred_element_type=jnp.float32
     )

time: 265 us -> 282 us (1.064)
  waiting for transfers between devices: 0.02 us -> 103 us
  blocking collectives: 226 us -> 126 us
  starting transfers between devices: 0.01 us -> 9.07 us
  local copies, waits for them, and re-layouts: 0.89 us -> 4.23 us
    all_to_all x1 -> x0, blocking collectives: 116 us -> none  [on_device(): lax.all_to_all(outgoing, 'exp', split_axis=0, concat_axis=0, tiled=True)]
    all_gather x1, waiting for transfers between devices: 0.01 us -> 65.4 us  [on_device(): stacked = lax.all_gather(stacked, 'rep', axis=2, tiled=True)]
    all_to_all x0 -> x1, waiting for transfers between devices: none -> 38.1 us  [on_device(): lax.all_to_all(outgoing, 'exp', split_axis=0, concat_axis=0, tiled=True)]
    all_to_all x1, blocking collectives: 110 us -> 126 us  [on_device(): lax.all_to_all(apply_experts(received, stacked), 'exp', split_axis=0, con...]
    all_to_all x0 -> x1, starting transfers between devices: none -> 9.06 us  [on_device(): lax.all_to_all(outgoing, 'exp', split_axis=0, concat_axis=0, tiled=True)]
    dot_general x1, matrix products: 9.35 us -> 4.3 us  [apply_experts(): lax.dot_general(hidden, weights[2, 0], (((1,), (1,)), ((), ())), preferre...]
    squeeze x0 -> x1, local copies, waits for them, and re-layouts: none -> 3.33 us  [apply_experts(): gate_up = jnp.concatenate([weights[0, 0], weights[1, 0]], axis=1)]
  transfers between devices with their start and end apart: 1 -> 2, of which waited for: 0 -> 2; matrix products, arithmetic and copies ran while one was open for 2% -> 4% of each run, Pallas kernels for 0% -> 0%
where the time goes in v4:
time: 282 us; the launch traced here: 279 us
  blocking collectives  126 us (45%)
  waiting for transfers between devices  103 us (37%)
  matrix products  16.8 us (6%)
  between operations  13.5 us (5%)
  starting transfers between devices  9.07 us (3%)
  other arithmetic  5.76 us (2%)
  local copies, waits for them, and re-layouts  4.23 us (2%)
    all_to_all x1, blocking collectives, on_device(): lax.all_to_all(apply_experts(received, stacked), 'exp', split_axis=0, con...  126 us
    all_gather x1, waiting for transfers between devices, on_device(): stacked = lax.all_gather(stacked, 'rep', axis=2, tiled=True)  65.4 us
    all_to_all x1, waiting for transfers between devices, on_device(): lax.all_to_all(outgoing, 'exp', split_axis=0, concat_axis=0, tiled=True)  38.1 us
    all_to_all x1, starting transfers between devices, on_device(): lax.all_to_all(outgoing, 'exp', split_axis=0, concat_axis=0, tiled=True)  9.06 us
    dot_general x1, matrix products, apply_experts(): both = jnp.dot(row_block, gate_up, preferred_element_type=jnp.float32)  6.13 us
  transfers between devices with their start and end apart: 2, of which 2 were waited for; matrix products, arithmetic and copies ran while one was open for 4% of the time, Pallas kernels for 0%

profile of v4, /device:TPU:6, one launch (start us, length us, event | category | flops | bytes accessed | tf_op | source)
XLA Modules:
  0.0 278.9 jit_solution(13502072474711836754)
XLA Ops:
  6.5 0.0 copy-start
  6.5 0.0 all-gather.2.cloned.1.call-start
  6.5 1.6 pad_maximum_fusion
  8.1 0.0 all-gather.2.cloned.1.call-update
  8.1 0.8 select_reduce_fusion.2
  9.0 0.1 fusion.10
  9.2 0.1 copy.16
  9.3 0.8 copy.17
  10.0 2.8 %select_reduce_fusion = (f32[128,1152]{1,0:T(8,128)S(1)}, bf16[128,1152]{1,0:T(8,128)(2,1)S(1)}) fusion(f32[128,8]{1,0:T(8,128)S(1)} %copy.17, s32[128,8]{1,0:T(8,128)S(1)} %copy.16), kind=kLoop, calls=%fused_computation.3 | loop fusion | flops 5603328 | bytes 892928 | tf_op jit(solution)/shard_map/reduce_sum | solution.py:55
  12.9 0.0 copy-done
  12.9 3.7 %convolution_convert_fusion.1 = bf16[1152,2048]{1,0:T(8,128)(2,1)} fusion(bf16[128,2048]{1,0:T(8,128)(2,1)S(1)} %copy-done, bf16[128,1152]{1,0:T(8,128)(2,1)S(1)} %get-tuple-element.6), kind=kOutput, calls=%fused_computation.1 | convolution fusion | flops 606339072 | bytes 5537792 | tf_op jit(solution)/shard_map/dot_general | solution.py:44
  16.6 9.1 %all-to-all-start = ((bf16[16,1,72,2048]{3,2,1,0:T(8,128)(2,1)}), bf16[16,1,72,2048]{3,2,1,0:T(8,128)(2,1)}, u32[]{:S(2)}, u32[]{:S(2)}) async-start(bf16[16,1,72,2048]{3,2,1,0:T(8,128)(2,1)} %bitcast.27), calls=%async_computation | async-start | bytes 9437184 | tf_op jit(solution)/shard_map/all_to_all | solution.py:50
  25.6 65.4 %all-gather.2.cloned.1.call-done = bf16[3,1,2048,384]{3,2,1,0:T(8,128)(2,1)} async-done(((bf16[3,1,64,384]{3,2,1,0:T(8,128)(2,1)}), bf16[3,1,2048,384]{3,2,1,0:T(8,128)(2,1)}) %all-gather.2.cloned.1.call-update) | async-done | bytes 4718608 | tf_op jit(solution)/shard_map/all_gather | solution.py:49
  91.0 3.3 %slice_bitcast_fusion.3 = (bf16[2048,384]{1,0:T(8,128)(2,1)S(1)}, bf16[2048,384]{1,0:T(8,128)(2,1)}) fusion(bf16[3,1,2048,384]{3,2,1,0:T(8,128)(2,1)} %all-gather.2.cloned.1.call-done), kind=kLoop, calls=%fused_computation.15 | loop fusion | bytes 6291456 | tf_op jit(solution)/shard_map/squeeze | solution.py:13
  94.4 38.1 %all-to-all-done = bf16[16,1,72,2048]{3,2,1,0:T(8,128)(2,1)} async-done(((bf16[16,1,72,2048]{3,2,1,0:T(8,128)(2,1)}), bf16[16,1,72,2048]{3,2,1,0:T(8,128)(2,1)}, u32[]{:S(2)}, u32[]{:S(2)}) %all-to-all-start) | async-done | bytes 4718624 | tf_op jit(solution)/shard_map/all_to_all | solution.py:50
  132.4 6.1 %fusion = f32[1152,768]{1,0:T(8,128)S(1)} fusion(bf16[1152,2048]{1,0:T(8,128)(2,1)} %bitcast.2, bf16[2048,384]{1,0:T(8,128)(2,1)} %get-tuple-element.8, bf16[2048,384]{1,0:T(8,128)(2,1)S(1)} %get-tuple-element.7), kind=kOutput, calls=%fused_computation.5 | convolution fusion | flops 3630170112 | bytes 11403264 | tf_op jit(solution)/shard_map/dot_general | solution.py:14
  138.6 0.5 fusion.5
  139.1 4.3 %convolution_convert_fusion = bf16[1152,2048]{1,0:T(8,128)(2,1)S(1)} fusion(bf16[1152,384]{1,0:T(8,128)(2,1)S(1)} %fusion.5, bf16[3,1,2048,384]{3,2,1,0:T(8,128)(2,1)} %all-gather.2.cloned.1.call-done), kind=kOutput, calls=%fused_computation | convolution fusion | flops 1814298624 | bytes 7176192 | tf_op jit(solution)/shard_map/dot_general | solution.py:18
  143.4 126.1 %all_to_all.10 = bf16[16,1,72,2048]{3,2,1,0:T(8,128)(2,1)S(1)} all-to-all(bf16[16,1,72,2048]{3,2,1,0:T(8,128)(2,1)S(1)} %bitcast.28), channel_id=1, replica_groups=mesh['rep'=32,'exp'=16] {'exp'}, dimensions={0} | all-to-all | bytes 9437184 | tf_op jit(solution)/shard_map/all_to_all | solution.py:51
  269.5 0.9 fusion.8
  270.4 1.7 fusion.4
  (3 shorter events, 0.1 us)
Async XLA Ops:
  6.5 6.4 %copy-start = (bf16[128,2048]{1,0:T(8,128)(2,1)S(1)}, bf16[128,2048]{1,0:T(8,128)(2,1)}, u32[]{:S(2)}) copy-start(bf16[128,2048]{1,0:T(8,128)(2,1)} %param.7) | copy-start | bytes 1572868
  6.5 84.5 %all-gather.2.cloned.1.call-start = ((), (), s32[]{:S(2)}) async-start(), calls=%async_computation.2 | async-start | bytes 4866048 | tf_op jit(solution)/shard_map/all_gather | solution.py:49
  16.6 115.9 %all-to-all-start = ((bf16[16,1,72,2048]{3,2,1,0:T(8,128)(2,1)}), bf16[16,1,72,2048]{3,2,1,0:T(8,128)(2,1)}, u32[]{:S(2)}, u32[]{:S(2)}) async-start(bf16[16,1,72,2048]{3,2,1,0:T(8,128)(2,1)} %bitcast.27), calls=%async_computation | async-start | bytes 9437184 | tf_op jit(solution)/shard_map/all_to_all | solution.py:50
Sparse Core Ops, SparseCore 0:
  10.5 80.4 all-gather.1

commit v5 on v1

--- a/solution.py
+++ b/solution.py
@@ -43,7 +43,17 @@
     ).astype(jnp.bfloat16)
     outgoing = outgoing.reshape(groups, local_experts, CAP, model_width)
     stacked = jnp.stack([w_gate, w_up, down_rows])
-    stacked = lax.all_gather(stacked, "rep", axis=2, tiled=True)
+    copies = lax.axis_size("rep")
+    me = lax.axis_index("rep")
+    pieces = [stacked]
+    for shift in range(1, copies):
+        pairs = [(i, (i + shift) % copies) for i in range(copies)]
+        pieces.append(lax.ppermute(stacked, "rep", pairs))
+    ordered = jnp.stack(pieces)
+    order = (me - jnp.arange(copies, dtype=jnp.int32)) % copies
+    inverse = jnp.zeros((copies,), jnp.int32).at[order].set(jnp.arange(copies, dtype=jnp.int32))
+    ordered = jnp.take(ordered, inverse, axis=0)
+    stacked = jnp.moveaxis(ordered, 0, 2).reshape(3, 1, -1, stacked.shape[-1])
     received = lax.all_to_all(outgoing, "exp", split_axis=0, concat_axis=0, tiled=True)
     returned = lax.all_to_all(
         apply_experts(received, stacked), "exp", split_axis=0, concat_axis=0, tiled=True

time: 265 us -> 389 us (1.47)
  starting transfers between devices: 0.01 us -> 191 us
  blocking collectives: 226 us -> 112 us
  local copies, waits for them, and re-layouts: 0.89 us -> 30.4 us
  waiting for transfers between devices: 0.02 us -> 23 us
  between operations: 13.5 us -> 0.42 us
    ppermute x0 -> x31, starting transfers between devices: none -> 182 us  [on_device(): pieces.append(lax.ppermute(stacked, 'rep', pairs))]
    all_to_all x1 -> x0, blocking collectives: 116 us -> none  [on_device(): lax.all_to_all(outgoing, 'exp', split_axis=0, concat_axis=0, tiled=True)]
    ppermute x0 -> x31, waiting for transfers between devices: none -> 23 us  [on_device(): pieces.append(lax.ppermute(stacked, 'rep', pairs))]
    unnamed x3 -> x39, local copies, waits for them, and re-layouts: 0.79 us -> 21 us
    all_to_all x0 -> x1, starting transfers between devices: none -> 9.19 us  [on_device(): lax.all_to_all(outgoing, 'exp', split_axis=0, concat_axis=0, tiled=True)]
    gather x0 -> x1, local copies, waits for them, and re-layouts: none -> 5.66 us  [on_device(): ordered = jnp.take(ordered, inverse, axis=0)]
  transfers between devices with their start and end apart: 1 -> 32, of which waited for: 0 -> 5; matrix products, arithmetic and copies ran while one was open for 2% -> 9% of each run, Pallas kernels for 0% -> 0%
where the time goes in v5:
time: 389 us; the launch traced here: 386 us
  starting transfers between devices  191 us (49%)
  blocking collectives  112 us (29%)
  local copies, waits for them, and re-layouts  30.4 us (8%)
  waiting for transfers between devices  23 us (6%)
  matrix products  22.1 us (6%)
  other arithmetic  7.42 us (2%)
    ppermute x31, starting transfers between devices, on_device(): pieces.append(lax.ppermute(stacked, 'rep', pairs))  182 us
    all_to_all x1, blocking collectives, on_device(): lax.all_to_all(apply_experts(received, stacked), 'exp', split_axis=0, con...  112 us
    ppermute x31, waiting for transfers between devices, on_device(): pieces.append(lax.ppermute(stacked, 'rep', pairs))  23 us
    unnamed x39, local copies, waits for them, and re-layouts  21 us
    all_to_all x1, starting transfers between devices, on_device(): lax.all_to_all(outgoing, 'exp', split_axis=0, concat_axis=0, tiled=True)  9.19 us
    dot_general x1, matrix products, apply_experts(): lax.dot_general(hidden, weights[2, 0], (((1,), (1,)), ((), ())), preferre...  9.11 us
  transfers between devices with their start and end apart: 32, of which 5 were waited for; matrix products, arithmetic and copies ran while one was open for 9% of the time, Pallas kernels for 0%

profile of v5, /device:TPU:6, one launch (start us, length us, event | category | flops | bytes accessed | tf_op | source)
XLA Modules:
  0.0 385.7 jit_solution(9001698573838071278)
XLA Ops:
  2.0 2.8 select_reduce_fusion
  4.8 3.6 convolution_convert_fusion.1
  8.4 9.2 %all-to-all-start = ((bf16[16,1,72,2048]{3,2,1,0:T(8,128)(2,1)}), bf16[16,1,72,2048]{3,2,1,0:T(8,128)(2,1)}, u32[]{:S(2)}, u32[]{:S(2)}) async-start(bf16[16,1,72,2048]{3,2,1,0:T(8,128)(2,1)} %bitcast.130), calls=%async_computation | async-start | bytes 9437184 | tf_op jit(solution)/shard_map/all_to_all | solution.py:57
  19.6 6.0 %collective-permute-start.1 = (bf16[3,1,64,384]{3,2,0,1:T(8,128)(2,1)S(1)}, bf16[3,1,64,384]{3,2,0,1:T(8,128)(2,1)S(1)}, u32[]{:S(2)}, u32[]{:S(2)}) collective-permute-start(bf16[3,1,64,384]{3,2,0,1:T(8,128)(2,1)S(1)} %get-tuple-element.11), channel_id=1, source_target_pairs={{0,32},{16,48},{32,64},{48,80},{64,96},{80,112},{96,128},{112,144}... | collective-permute-start | bytes 442376 | tf_op jit(solution)/shard_map/ppermute | solution.py:51
  25.6 4.3 %collective-permute-start.2 = (bf16[3,1,64,384]{3,2,0,1:T(8,128)(2,1)S(1)}, bf16[3,1,64,384]{3,2,0,1:T(8,128)(2,1)S(1)}, u32[]{:S(2)}, u32[]{:S(2)}) collective-permute-start(bf16[3,1,64,384]{3,2,0,1:T(8,128)(2,1)S(1)} %get-tuple-element.11), channel_id=1, source_target_pairs={{0,48},{16,64},{32,80},{48,96},{64,112},{80,128},{96,144},{112,160... | collective-permute-start | bytes 442376 | tf_op jit(solution)/shard_map/ppermute | solution.py:51
  29.9 7.0 %collective-permute-start.3 = (bf16[3,1,64,384]{3,2,0,1:T(8,128)(2,1)S(1)}, bf16[3,1,64,384]{3,2,0,1:T(8,128)(2,1)S(1)}, u32[]{:S(2)}, u32[]{:S(2)}) collective-permute-start(bf16[3,1,64,384]{3,2,0,1:T(8,128)(2,1)S(1)} %get-tuple-element.11), channel_id=1, source_target_pairs={{0,64},{16,80},{32,96},{48,112},{64,128},{80,144},{96,160},{112,17... | collective-permute-start | bytes 442376 | tf_op jit(solution)/shard_map/ppermute | solution.py:51
  36.9 3.8 collective-permute-start.4
  42.1 3.6 collective-permute-start.5
  52.4 15.4 %collective-permute-start.8 = (bf16[3,1,64,384]{3,2,0,1:T(8,128)(2,1)S(1)}, bf16[3,1,64,384]{3,2,0,1:T(8,128)(2,1)S(1)}, u32[]{:S(2)}, u32[]{:S(2)}) collective-permute-start(bf16[3,1,64,384]{3,2,0,1:T(8,128)(2,1)S(1)} %get-tuple-element.11), channel_id=1, source_target_pairs={{0,144},{16,160},{32,176},{48,192},{64,208},{80,224},{96,240},{112... | collective-permute-start | bytes 442376 | tf_op jit(solution)/shard_map/ppermute | solution.py:51
  73.5 9.2 %collective-permute-start.10 = (bf16[3,1,64,384]{3,2,0,1:T(8,128)(2,1)S(1)}, bf16[3,1,64,384]{3,2,0,1:T(8,128)(2,1)S(1)}, u32[]{:S(2)}, u32[]{:S(2)}) collective-permute-start(bf16[3,1,64,384]{3,2,0,1:T(8,128)(2,1)S(1)} %get-tuple-element.11), channel_id=1, source_target_pairs={{0,176},{16,192},{32,208},{48,224},{64,240},{80,256},{96,272},{112... | collective-permute-start | bytes 442376 | tf_op jit(solution)/shard_map/ppermute | solution.py:51
  85.1 6.5 %collective-permute-start.11 = (bf16[3,1,64,384]{3,2,0,1:T(8,128)(2,1)S(1)}, bf16[3,1,64,384]{3,2,0,1:T(8,128)(2,1)S(1)}, u32[]{:S(2)}, u32[]{:S(2)}) collective-permute-start(bf16[3,1,64,384]{3,2,0,1:T(8,128)(2,1)S(1)} %get-tuple-element.11), channel_id=1, source_target_pairs={{0,192},{16,208},{32,224},{48,240},{64,256},{80,272},{96,288},{112... | collective-permute-start | bytes 442376 | tf_op jit(solution)/shard_map/ppermute | solution.py:51
  92.4 6.0 %collective-permute-start.12 = (bf16[3,1,64,384]{3,2,0,1:T(8,128)(2,1)S(1)}, bf16[3,1,64,384]{3,2,0,1:T(8,128)(2,1)S(1)}, u32[]{:S(2)}, u32[]{:S(2)}) collective-permute-start(bf16[3,1,64,384]{3,2,0,1:T(8,128)(2,1)S(1)} %get-tuple-element.11), channel_id=1, source_target_pairs={{0,208},{16,224},{32,240},{48,256},{64,272},{80,288},{96,304},{112... | collective-permute-start | bytes 442376 | tf_op jit(solution)/shard_map/ppermute | solution.py:51
  99.1 11.8 %collective-permute-start.13 = (bf16[3,1,64,384]{3,2,0,1:T(8,128)(2,1)S(1)}, bf16[3,1,64,384]{3,2,0,1:T(8,128)(2,1)S(1)}, u32[]{:S(2)}, u32[]{:S(2)}) collective-permute-start(bf16[3,1,64,384]{3,2,0,1:T(8,128)(2,1)S(1)} %get-tuple-element.11), channel_id=1, source_target_pairs={{0,224},{16,240},{32,256},{48,272},{64,288},{80,304},{96,320},{112... | collective-permute-start | bytes 442376 | tf_op jit(solution)/shard_map/ppermute | solution.py:51
  114.1 14.4 %collective-permute-done.10 = bf16[3,1,64,384]{3,2,0,1:T(8,128)(2,1)S(1)} collective-permute-done((bf16[3,1,64,384]{3,2,0,1:T(8,128)(2,1)S(1)}, bf16[3,1,64,384]{3,2,0,1:T(8,128)(2,1)S(1)}, u32[]{:S(2)}, u32[]{:S(2)}) %collective-permute-start.10) | collective-permute-done | bytes 147488 | tf_op jit(solution)/shard_map/ppermute | solution.py:51
  128.5 10.6 %collective-permute-start.15 = (bf16[3,1,64,384]{3,2,0,1:T(8,128)(2,1)S(1)}, bf16[3,1,64,384]{3,2,0,1:T(8,128)(2,1)S(1)}, u32[]{:S(2)}, u32[]{:S(2)}) collective-permute-start(bf16[3,1,64,384]{3,2,0,1:T(8,128)(2,1)S(1)} %get-tuple-element.11), channel_id=1, source_target_pairs={{0,256},{16,272},{32,288},{48,304},{64,320},{80,336},{96,352},{112... | collective-permute-start | bytes 442376 | tf_op jit(solution)/shard_map/ppermute | solution.py:51
  139.8 2.5 collective-permute-done.11
  142.3 4.7 %collective-permute-start.16 = (bf16[3,1,64,384]{3,2,0,1:T(8,128)(2,1)S(1)}, bf16[3,1,64,384]{3,2,0,1:T(8,128)(2,1)S(1)}, u32[]{:S(2)}, u32[]{:S(2)}) collective-permute-start(bf16[3,1,64,384]{3,2,0,1:T(8,128)(2,1)S(1)} %get-tuple-element.11), channel_id=1, source_target_pairs={{0,272},{16,288},{32,304},{48,320},{64,336},{80,352},{96,368},{112... | collective-permute-start | bytes 442376 | tf_op jit(solution)/shard_map/ppermute | solution.py:51
  147.7 31.4 %collective-permute-start.17 = (bf16[3,1,64,384]{3,2,0,1:T(8,128)(2,1)S(1)}, bf16[3,1,64,384]{3,2,0,1:T(8,128)(2,1)S(1)}, u32[]{:S(2)}, u32[]{:S(2)}) collective-permute-start(bf16[3,1,64,384]{3,2,0,1:T(8,128)(2,1)S(1)} %get-tuple-element.11), channel_id=1, source_target_pairs={{0,288},{16,304},{32,320},{48,336},{64,352},{80,368},{96,384},{112... | collective-permute-start | bytes 442376 | tf_op jit(solution)/shard_map/ppermute | solution.py:51
  179.8 3.4 collective-permute-start.18
  186.5 4.0 %collective-permute-start.20 = (bf16[3,1,64,384]{3,2,0,1:T(8,128)(2,1)S(1)}, bf16[3,1,64,384]{3,2,0,1:T(8,128)(2,1)S(1)}, u32[]{:S(2)}, u32[]{:S(2)}) collective-permute-start(bf16[3,1,64,384]{3,2,0,1:T(8,128)(2,1)S(1)} %get-tuple-element.11), channel_id=1, source_target_pairs={{0,336},{16,352},{32,368},{48,384},{64,400},{80,416},{96,432},{112... | collective-permute-start | bytes 442376 | tf_op jit(solution)/shard_map/ppermute | solution.py:51
  191.2 12.4 %collective-permute-start.21 = (bf16[3,1,64,384]{3,2,0,1:T(8,128)(2,1)S(1)}, bf16[3,1,64,384]{3,2,0,1:T(8,128)(2,1)S(1)}, u32[]{:S(2)}, u32[]{:S(2)}) collective-permute-start(bf16[3,1,64,384]{3,2,0,1:T(8,128)(2,1)S(1)} %get-tuple-element.11), channel_id=1, source_target_pairs={{0,352},{16,368},{32,384},{48,400},{64,416},{80,432},{96,448},{112... | collective-permute-start | bytes 442376 | tf_op jit(solution)/shard_map/ppermute | solution.py:51
  206.9 4.7 %collective-permute-start.23 = (bf16[3,1,64,384]{3,2,0,1:T(8,128)(2,1)S(1)}, bf16[3,1,64,384]{3,2,0,1:T(8,128)(2,1)S(1)}, u32[]{:S(2)}, u32[]{:S(2)}) collective-permute-start(bf16[3,1,64,384]{3,2,0,1:T(8,128)(2,1)S(1)} %get-tuple-element.11), channel_id=1, source_target_pairs={{0,384},{16,400},{32,416},{48,432},{64,448},{80,464},{96,480},{112... | collective-permute-start | bytes 442376 | tf_op jit(solution)/shard_map/ppermute | solution.py:51
  214.9 3.4 collective-permute-start.25
  218.9 2.8 collective-permute-start.26
  222.4 5.9 %collective-permute-start.27 = (bf16[3,1,64,384]{3,2,0,1:T(8,128)(2,1)S(1)}, bf16[3,1,64,384]{3,2,0,1:T(8,128)(2,1)S(1)}, u32[]{:S(2)}, u32[]{:S(2)}) collective-permute-start(bf16[3,1,64,384]{3,2,0,1:T(8,128)(2,1)S(1)} %get-tuple-element.11), channel_id=1, source_target_pairs={{0,448},{16,464},{32,480},{48,496},{64,0},{80,16},{96,32},{112,48}... | collective-permute-start | bytes 442376 | tf_op jit(solution)/shard_map/ppermute | solution.py:51
  229.0 3.7 collective-permute-start.28
  236.2 2.8 collective-permute-start.30
  244.8 5.7 %gather_fusion = bf16[32,3,64,384]{3,2,1,0:T(8,128)(2,1)} fusion(bf16[32,3,64,384]{3,2,1,0:T(8,128)(2,1)} %bitcast.69, s32[1024]{0:T(1024)S(1)} %pad_clamp_fusion), kind=kCustom, calls=%fused_computation | custom fusion | bytes 9437312 | tf_op jit(solution)/shard_map/jit(_take)/gather | solution.py:55
  250.5 2.9 fusion
  255.7 6.6 %fusion.16 = f32[1152,384]{1,0:T(8,128)} fusion(bf16[1152,2048]{1,0:T(8,128)(2,1)} %bitcast.2, bf16[2048,384]{1,0:T(8,128)(2,1)} %bitcast.134), kind=kOutput, calls=%fused_computation.74 | convolution fusion | flops 1811939328 | bytes 8060928 | tf_op jit(solution)/shard_map/dot_general | solution.py:12
  262.4 9.1 %convolution_convert_fusion = bf16[1152,2048]{1,0:T(8,128)(2,1)} fusion(bf16[2048,384]{1,0:T(8,128)(2,1)S(1)} %bitcast.132, bf16[1152,2048]{1,0:T(8,128)(2,1)} %bitcast.2, bf16[2048,384]{1,0:T(8,128)(2,1)} %bitcast.133, f32[1152,384]{1,0:T(8,128)} %fusion.16), kind=kOutput, calls=%fused_computation.2 | convolution fusion | flops 3628892160 | bytes 14352384 | tf_op jit(solution)/shard_map/dot_general | solution.py:15
  271.5 111.7 %all_to_all.10 = bf16[16,1,72,2048]{3,2,1,0:T(8,128)(2,1)S(1)} all-to-all(bf16[16,1,72,2048]{3,2,1,0:T(8,128)(2,1)} %bitcast.131), channel_id=1, replica_groups=mesh['rep'=32,'exp'=16] {'exp'}, dimensions={0} | all-to-all | bytes 9437184 | tf_op jit(solution)/shard_map/all_to_all | solution.py:58
  (96 shorter events, 53.3 us)
Async XLA Ops:
  8.4 247.3 %all-to-all-start = ((bf16[16,1,72,2048]{3,2,1,0:T(8,128)(2,1)}), bf16[16,1,72,2048]{3,2,1,0:T(8,128)(2,1)}, u32[]{:S(2)}, u32[]{:S(2)}) async-start(bf16[16,1,72,2048]{3,2,1,0:T(8,128)(2,1)} %bitcast.130), calls=%async_computation | async-start | bytes 9437184 | tf_op jit(solution)/shard_map/all_to_all | solution.py:57
  17.7 24.4 %collective-permute-start = (bf16[3,1,64,384]{3,2,0,1:T(8,128)(2,1)S(1)}, bf16[3,1,64,384]{3,2,0,1:T(8,128)(2,1)S(1)}, u32[]{:S(2)}, u32[]{:S(2)}) collective-permute-start(bf16[3,1,64,384]{3,2,0,1:T(8,128)(2,1)S(1)} %get-tuple-element.11), channel_id=1, source_target_pairs={{0,16},{16,32},{32,48},{48,64},{64,80},{80,96},{96,112},{112,128},... | collective-permute-start | bytes 442376 | tf_op jit(solution)/shard_map/ppermute | solution.py:51
  19.6 26.8 %collective-permute-start.1 = (bf16[3,1,64,384]{3,2,0,1:T(8,128)(2,1)S(1)}, bf16[3,1,64,384]{3,2,0,1:T(8,128)(2,1)S(1)}, u32[]{:S(2)}, u32[]{:S(2)}) collective-permute-start(bf16[3,1,64,384]{3,2,0,1:T(8,128)(2,1)S(1)} %get-tuple-element.11), channel_id=1, source_target_pairs={{0,32},{16,48},{32,64},{48,80},{64,96},{80,112},{96,128},{112,144}... | collective-permute-start | bytes 442376 | tf_op jit(solution)/shard_map/ppermute | solution.py:51
  25.6 23.7 %collective-permute-start.2 = (bf16[3,1,64,384]{3,2,0,1:T(8,128)(2,1)S(1)}, bf16[3,1,64,384]{3,2,0,1:T(8,128)(2,1)S(1)}, u32[]{:S(2)}, u32[]{:S(2)}) collective-permute-start(bf16[3,1,64,384]{3,2,0,1:T(8,128)(2,1)S(1)} %get-tuple-element.11), channel_id=1, source_target_pairs={{0,48},{16,64},{32,80},{48,96},{64,112},{80,128},{96,144},{112,160... | collective-permute-start | bytes 442376 | tf_op jit(solution)/shard_map/ppermute | solution.py:51
  29.9 22.5 %collective-permute-start.3 = (bf16[3,1,64,384]{3,2,0,1:T(8,128)(2,1)S(1)}, bf16[3,1,64,384]{3,2,0,1:T(8,128)(2,1)S(1)}, u32[]{:S(2)}, u32[]{:S(2)}) collective-permute-start(bf16[3,1,64,384]{3,2,0,1:T(8,128)(2,1)S(1)} %get-tuple-element.11), channel_id=1, source_target_pairs={{0,64},{16,80},{32,96},{48,112},{64,128},{80,144},{96,160},{112,17... | collective-permute-start | bytes 442376 | tf_op jit(solution)/shard_map/ppermute | solution.py:51
  36.9 31.6 %collective-permute-start.4 = (bf16[3,1,64,384]{3,2,0,1:T(8,128)(2,1)S(1)}, bf16[3,1,64,384]{3,2,0,1:T(8,128)(2,1)S(1)}, u32[]{:S(2)}, u32[]{:S(2)}) collective-permute-start(bf16[3,1,64,384]{3,2,0,1:T(8,128)(2,1)S(1)} %get-tuple-element.11), channel_id=1, source_target_pairs={{0,80},{16,96},{32,112},{48,128},{64,144},{80,160},{96,176},{112,1... | collective-permute-start | bytes 442376 | tf_op jit(solution)/shard_map/ppermute | solution.py:51
  42.1 31.4 %collective-permute-start.5 = (bf16[3,1,64,384]{3,2,0,1:T(8,128)(2,1)S(1)}, bf16[3,1,64,384]{3,2,0,1:T(8,128)(2,1)S(1)}, u32[]{:S(2)}, u32[]{:S(2)}) collective-permute-start(bf16[3,1,64,384]{3,2,0,1:T(8,128)(2,1)S(1)} %get-tuple-element.11), channel_id=1, source_target_pairs={{0,96},{16,112},{32,128},{48,144},{64,160},{80,176},{96,192},{112,... | collective-permute-start | bytes 442376 | tf_op jit(solution)/shard_map/ppermute | solution.py:51
  46.5 38.7 %collective-permute-start.6 = (bf16[3,1,64,384]{3,2,0,1:T(8,128)(2,1)S(1)}, bf16[3,1,64,384]{3,2,0,1:T(8,128)(2,1)S(1)}, u32[]{:S(2)}, u32[]{:S(2)}) collective-permute-start(bf16[3,1,64,384]{3,2,0,1:T(8,128)(2,1)S(1)} %get-tuple-element.11), channel_id=1, source_target_pairs={{0,112},{16,128},{32,144},{48,160},{64,176},{80,192},{96,208},{112... | collective-permute-start | bytes 442376 | tf_op jit(solution)/shard_map/ppermute | solution.py:51
  49.3 43.0 %collective-permute-start.7 = (bf16[3,1,64,384]{3,2,0,1:T(8,128)(2,1)S(1)}, bf16[3,1,64,384]{3,2,0,1:T(8,128)(2,1)S(1)}, u32[]{:S(2)}, u32[]{:S(2)}) collective-permute-start(bf16[3,1,64,384]{3,2,0,1:T(8,128)(2,1)S(1)} %get-tuple-element.11), channel_id=1, source_target_pairs={{0,128},{16,144},{32,160},{48,176},{64,192},{80,208},{96,224},{112... | collective-permute-start | bytes 442376 | tf_op jit(solution)/shard_map/ppermute | solution.py:51
  52.4 46.7 %collective-permute-start.8 = (bf16[3,1,64,384]{3,2,0,1:T(8,128)(2,1)S(1)}, bf16[3,1,64,384]{3,2,0,1:T(8,128)(2,1)S(1)}, u32[]{:S(2)}, u32[]{:S(2)}) collective-permute-start(bf16[3,1,64,384]{3,2,0,1:T(8,128)(2,1)S(1)} %get-tuple-element.11), channel_id=1, source_target_pairs={{0,144},{16,160},{32,176},{48,192},{64,208},{80,224},{96,240},{112... | collective-permute-start | bytes 442376 | tf_op jit(solution)/shard_map/ppermute | solution.py:51
  68.5 43.0 %collective-permute-start.9 = (bf16[3,1,64,384]{3,2,0,1:T(8,128)(2,1)S(1)}, bf16[3,1,64,384]{3,2,0,1:T(8,128)(2,1)S(1)}, u32[]{:S(2)}, u32[]{:S(2)}) collective-permute-start(bf16[3,1,64,384]{3,2,0,1:T(8,128)(2,1)S(1)} %get-tuple-element.11), channel_id=1, source_target_pairs={{0,160},{16,176},{32,192},{48,208},{64,224},{80,240},{96,256},{112... | collective-permute-start | bytes 442376 | tf_op jit(solution)/shard_map/ppermute | solution.py:51
  73.5 55.0 %collective-permute-start.10 = (bf16[3,1,64,384]{3,2,0,1:T(8,128)(2,1)S(1)}, bf16[3,1,64,384]{3,2,0,1:T(8,128)(2,1)S(1)}, u32[]{:S(2)}, u32[]{:S(2)}) collective-permute-start(bf16[3,1,64,384]{3,2,0,1:T(8,128)(2,1)S(1)} %get-tuple-element.11), channel_id=1, source_target_pairs={{0,176},{16,192},{32,208},{48,224},{64,240},{80,256},{96,272},{112... | collective-permute-start | bytes 442376 | tf_op jit(solution)/shard_map/ppermute | solution.py:51
  85.1 57.2 %collective-permute-start.11 = (bf16[3,1,64,384]{3,2,0,1:T(8,128)(2,1)S(1)}, bf16[3,1,64,384]{3,2,0,1:T(8,128)(2,1)S(1)}, u32[]{:S(2)}, u32[]{:S(2)}) collective-permute-start(bf16[3,1,64,384]{3,2,0,1:T(8,128)(2,1)S(1)} %get-tuple-element.11), channel_id=1, source_target_pairs={{0,192},{16,208},{32,224},{48,240},{64,256},{80,272},{96,288},{112... | collective-permute-start | bytes 442376 | tf_op jit(solution)/shard_map/ppermute | solution.py:51
  92.4 55.4 %collective-permute-start.12 = (bf16[3,1,64,384]{3,2,0,1:T(8,128)(2,1)S(1)}, bf16[3,1,64,384]{3,2,0,1:T(8,128)(2,1)S(1)}, u32[]{:S(2)}, u32[]{:S(2)}) collective-permute-start(bf16[3,1,64,384]{3,2,0,1:T(8,128)(2,1)S(1)} %get-tuple-element.11), channel_id=1, source_target_pairs={{0,208},{16,224},{32,240},{48,256},{64,272},{80,288},{96,304},{112... | collective-permute-start | bytes 442376 | tf_op jit(solution)/shard_map/ppermute | solution.py:51
  99.1 80.8 %collective-permute-start.13 = (bf16[3,1,64,384]{3,2,0,1:T(8,128)(2,1)S(1)}, bf16[3,1,64,384]{3,2,0,1:T(8,128)(2,1)S(1)}, u32[]{:S(2)}, u32[]{:S(2)}) collective-permute-start(bf16[3,1,64,384]{3,2,0,1:T(8,128)(2,1)S(1)} %get-tuple-element.11), channel_id=1, source_target_pairs={{0,224},{16,240},{32,256},{48,272},{64,288},{80,304},{96,320},{112... | collective-permute-start | bytes 442376 | tf_op jit(solution)/shard_map/ppermute | solution.py:51
  111.5 72.4 %collective-permute-start.14 = (bf16[3,1,64,384]{3,2,0,1:T(8,128)(2,1)S(1)}, bf16[3,1,64,384]{3,2,0,1:T(8,128)(2,1)S(1)}, u32[]{:S(2)}, u32[]{:S(2)}) collective-permute-start(bf16[3,1,64,384]{3,2,0,1:T(8,128)(2,1)S(1)} %get-tuple-element.11), channel_id=1, source_target_pairs={{0,240},{16,256},{32,272},{48,288},{64,304},{80,320},{96,336},{112... | collective-permute-start | bytes 442376 | tf_op jit(solution)/shard_map/ppermute | solution.py:51
  128.5 58.0 %collective-permute-start.15 = (bf16[3,1,64,384]{3,2,0,1:T(8,128)(2,1)S(1)}, bf16[3,1,64,384]{3,2,0,1:T(8,128)(2,1)S(1)}, u32[]{:S(2)}, u32[]{:S(2)}) collective-permute-start(bf16[3,1,64,384]{3,2,0,1:T(8,128)(2,1)S(1)} %get-tuple-element.11), channel_id=1, source_target_pairs={{0,256},{16,272},{32,288},{48,304},{64,320},{80,336},{96,352},{112... | collective-permute-start | bytes 442376 | tf_op jit(solution)/shard_map/ppermute | solution.py:51
  142.3 48.9 %collective-permute-start.16 = (bf16[3,1,64,384]{3,2,0,1:T(8,128)(2,1)S(1)}, bf16[3,1,64,384]{3,2,0,1:T(8,128)(2,1)S(1)}, u32[]{:S(2)}, u32[]{:S(2)}) collective-permute-start(bf16[3,1,64,384]{3,2,0,1:T(8,128)(2,1)S(1)} %get-tuple-element.11), channel_id=1, source_target_pairs={{0,272},{16,288},{32,304},{48,320},{64,336},{80,352},{96,368},{112... | collective-permute-start | bytes 442376 | tf_op jit(solution)/shard_map/ppermute | solution.py:51
  147.7 56.6 %collective-permute-start.17 = (bf16[3,1,64,384]{3,2,0,1:T(8,128)(2,1)S(1)}, bf16[3,1,64,384]{3,2,0,1:T(8,128)(2,1)S(1)}, u32[]{:S(2)}, u32[]{:S(2)}) collective-permute-start(bf16[3,1,64,384]{3,2,0,1:T(8,128)(2,1)S(1)} %get-tuple-element.11), channel_id=1, source_target_pairs={{0,288},{16,304},{32,320},{48,336},{64,352},{80,368},{96,384},{112... | collective-permute-start | bytes 442376 | tf_op jit(solution)/shard_map/ppermute | solution.py:51
  179.8 27.0 %collective-permute-start.18 = (bf16[3,1,64,384]{3,2,0,1:T(8,128)(2,1)S(1)}, bf16[3,1,64,384]{3,2,0,1:T(8,128)(2,1)S(1)}, u32[]{:S(2)}, u32[]{:S(2)}) collective-permute-start(bf16[3,1,64,384]{3,2,0,1:T(8,128)(2,1)S(1)} %get-tuple-element.11), channel_id=1, source_target_pairs={{0,304},{16,320},{32,336},{48,352},{64,368},{80,384},{96,400},{112... | collective-permute-start | bytes 442376 | tf_op jit(solution)/shard_map/ppermute | solution.py:51
  183.9 28.3 %collective-permute-start.19 = (bf16[3,1,64,384]{3,2,0,1:T(8,128)(2,1)S(1)}, bf16[3,1,64,384]{3,2,0,1:T(8,128)(2,1)S(1)}, u32[]{:S(2)}, u32[]{:S(2)}) collective-permute-start(bf16[3,1,64,384]{3,2,0,1:T(8,128)(2,1)S(1)} %get-tuple-element.11), channel_id=1, source_target_pairs={{0,320},{16,336},{32,352},{48,368},{64,384},{80,400},{96,416},{112... | collective-permute-start | bytes 442376 | tf_op jit(solution)/shard_map/ppermute | solution.py:51
  186.5 28.3 %collective-permute-start.20 = (bf16[3,1,64,384]{3,2,0,1:T(8,128)(2,1)S(1)}, bf16[3,1,64,384]{3,2,0,1:T(8,128)(2,1)S(1)}, u32[]{:S(2)}, u32[]{:S(2)}) collective-permute-start(bf16[3,1,64,384]{3,2,0,1:T(8,128)(2,1)S(1)} %get-tuple-element.11), channel_id=1, source_target_pairs={{0,336},{16,352},{32,368},{48,384},{64,400},{80,416},{96,432},{112... | collective-permute-start | bytes 442376 | tf_op jit(solution)/shard_map/ppermute | solution.py:51
  191.2 27.8 %collective-permute-start.21 = (bf16[3,1,64,384]{3,2,0,1:T(8,128)(2,1)S(1)}, bf16[3,1,64,384]{3,2,0,1:T(8,128)(2,1)S(1)}, u32[]{:S(2)}, u32[]{:S(2)}) collective-permute-start(bf16[3,1,64,384]{3,2,0,1:T(8,128)(2,1)S(1)} %get-tuple-element.11), channel_id=1, source_target_pairs={{0,352},{16,368},{32,384},{48,400},{64,416},{80,432},{96,448},{112... | collective-permute-start | bytes 442376 | tf_op jit(solution)/shard_map/ppermute | solution.py:51
  204.3 18.1 %collective-permute-start.22 = (bf16[3,1,64,384]{3,2,0,1:T(8,128)(2,1)S(1)}, bf16[3,1,64,384]{3,2,0,1:T(8,128)(2,1)S(1)}, u32[]{:S(2)}, u32[]{:S(2)}) collective-permute-start(bf16[3,1,64,384]{3,2,0,1:T(8,128)(2,1)S(1)} %get-tuple-element.11), channel_id=1, source_target_pairs={{0,368},{16,384},{32,400},{48,416},{64,432},{80,448},{96,464},{112... | collective-permute-start | bytes 442376 | tf_op jit(solution)/shard_map/ppermute | solution.py:51
  206.9 22.1 %collective-permute-start.23 = (bf16[3,1,64,384]{3,2,0,1:T(8,128)(2,1)S(1)}, bf16[3,1,64,384]{3,2,0,1:T(8,128)(2,1)S(1)}, u32[]{:S(2)}, u32[]{:S(2)}) collective-permute-start(bf16[3,1,64,384]{3,2,0,1:T(8,128)(2,1)S(1)} %get-tuple-element.11), channel_id=1, source_target_pairs={{0,384},{16,400},{32,416},{48,432},{64,448},{80,464},{96,480},{112... | collective-permute-start | bytes 442376 | tf_op jit(solution)/shard_map/ppermute | solution.py:51
  212.3 21.2 %collective-permute-start.24 = (bf16[3,1,64,384]{3,2,0,1:T(8,128)(2,1)S(1)}, bf16[3,1,64,384]{3,2,0,1:T(8,128)(2,1)S(1)}, u32[]{:S(2)}, u32[]{:S(2)}) collective-permute-start(bf16[3,1,64,384]{3,2,0,1:T(8,128)(2,1)S(1)} %get-tuple-element.11), channel_id=1, source_target_pairs={{0,400},{16,416},{32,432},{48,448},{64,464},{80,480},{96,496},{112... | collective-permute-start | bytes 442376 | tf_op jit(solution)/shard_map/ppermute | solution.py:51
  214.9 21.4 %collective-permute-start.25 = (bf16[3,1,64,384]{3,2,0,1:T(8,128)(2,1)S(1)}, bf16[3,1,64,384]{3,2,0,1:T(8,128)(2,1)S(1)}, u32[]{:S(2)}, u32[]{:S(2)}) collective-permute-start(bf16[3,1,64,384]{3,2,0,1:T(8,128)(2,1)S(1)} %get-tuple-element.11), channel_id=1, source_target_pairs={{0,416},{16,432},{32,448},{48,464},{64,480},{80,496},{96,0},{112,1... | collective-permute-start | bytes 442376 | tf_op jit(solution)/shard_map/ppermute | solution.py:51
  218.9 20.7 %collective-permute-start.26 = (bf16[3,1,64,384]{3,2,0,1:T(8,128)(2,1)S(1)}, bf16[3,1,64,384]{3,2,0,1:T(8,128)(2,1)S(1)}, u32[]{:S(2)}, u32[]{:S(2)}) collective-permute-start(bf16[3,1,64,384]{3,2,0,1:T(8,128)(2,1)S(1)} %get-tuple-element.11), channel_id=1, source_target_pairs={{0,432},{16,448},{32,464},{48,480},{64,496},{80,0},{96,16},{112,32... | collective-permute-start | bytes 442376 | tf_op jit(solution)/shard_map/ppermute | solution.py:51
  222.4 17.9 %collective-permute-start.27 = (bf16[3,1,64,384]{3,2,0,1:T(8,128)(2,1)S(1)}, bf16[3,1,64,384]{3,2,0,1:T(8,128)(2,1)S(1)}, u32[]{:S(2)}, u32[]{:S(2)}) collective-permute-start(bf16[3,1,64,384]{3,2,0,1:T(8,128)(2,1)S(1)} %get-tuple-element.11), channel_id=1, source_target_pairs={{0,448},{16,464},{32,480},{48,496},{64,0},{80,16},{96,32},{112,48}... | collective-permute-start | bytes 442376 | tf_op jit(solution)/shard_map/ppermute | solution.py:51
  229.0 12.0 %collective-permute-start.28 = (bf16[3,1,64,384]{3,2,0,1:T(8,128)(2,1)S(1)}, bf16[3,1,64,384]{3,2,0,1:T(8,128)(2,1)S(1)}, u32[]{:S(2)}, u32[]{:S(2)}) collective-permute-start(bf16[3,1,64,384]{3,2,0,1:T(8,128)(2,1)S(1)} %get-tuple-element.11), channel_id=1, source_target_pairs={{0,464},{16,480},{32,496},{48,0},{64,16},{80,32},{96,48},{112,64},... | collective-permute-start | bytes 442376 | tf_op jit(solution)/shard_map/ppermute | solution.py:51
  233.4 10.1 %collective-permute-start.29 = (bf16[3,1,64,384]{3,2,0,1:T(8,128)(2,1)S(1)}, bf16[3,1,64,384]{3,2,0,1:T(8,128)(2,1)S(1)}, u32[]{:S(2)}, u32[]{:S(2)}) collective-permute-start(bf16[3,1,64,384]{3,2,0,1:T(8,128)(2,1)S(1)} %get-tuple-element.11), channel_id=1, source_target_pairs={{0,480},{16,496},{32,0},{48,16},{64,32},{80,48},{96,64},{112,80},{... | collective-permute-start | bytes 442376 | tf_op jit(solution)/shard_map/ppermute | solution.py:51
  236.2 7.9 %collective-permute-start.30 = (bf16[3,1,64,384]{3,2,1,0:T(8,128)(2,1)S(1)}, bf16[3,1,64,384]{3,2,1,0:T(8,128)(2,1)S(1)}, u32[]{:S(2)}, u32[]{:S(2)}) collective-permute-start(bf16[3,1,64,384]{3,2,1,0:T(8,128)(2,1)S(1)} %get-tuple-element.10), channel_id=1, source_target_pairs={{0,496},{16,0},{32,16},{48,32},{64,48},{80,64},{96,80},{112,96},{1... | collective-permute-start | bytes 442376 | tf_op jit(solution)/shard_map/ppermute | solution.py:51
  (4 other events, 32.5 us)

commit v6 on v1

--- a/solution.py
+++ b/solution.py
@@ -36,8 +36,8 @@
     position = jnp.sum(jnp.where(slot_hot, before[:, None, :], 0.0), axis=2).astype(jnp.int32)
     target = slot_ids * CAP + position
     slot_range = jnp.arange(slots_total, dtype=jnp.int32)
-    hits = target[:, :, None] == slot_range
-    scatter = jnp.sum(hits.astype(jnp.float32), axis=1).astype(jnp.bfloat16)
+    hits = target.T[:, :, None] == slot_range
+    scatter = jnp.sum(hits.astype(jnp.float32), axis=0).astype(jnp.bfloat16)
     outgoing = lax.dot_general(
         scatter, tokens, (((0,), (0,)), ((), ())), preferred_element_type=jnp.float32
     ).astype(jnp.bfloat16)
@@ -49,7 +49,7 @@
         apply_experts(received, stacked), "exp", split_axis=0, concat_axis=0, tiled=True
     )
     returned = returned.reshape(slots_total, model_width)
-    combine = jnp.sum(jnp.where(hits, route_weights[:, :, None], 0.0), axis=1)
+    combine = jnp.sum(jnp.where(hits, route_weights.T[:, :, None], 0.0), axis=0)
     combine_hi = combine.astype(jnp.bfloat16)
     combine_lo = (combine - combine_hi.astype(jnp.float32)).astype(jnp.bfloat16)
     mixed = jnp.dot(combine_hi, returned, preferred_element_type=jnp.float32)

time: 265 us -> 263 us (level)
  no operation moved by 1% of the time
where the time goes in v6:
time: 263 us
  blocking collectives  226 us (86%)
  matrix products  18.4 us (7%)
  between operations  13.5 us (5%)
  other arithmetic  4.35 us (2%)
    all_to_all x1, blocking collectives, on_device(): lax.all_to_all(outgoing, 'exp', split_axis=0, concat_axis=0, tiled=True)  116 us
    all_to_all x1, blocking collectives, on_device(): lax.all_to_all(apply_experts(received, stacked), 'exp', split_axis=0, con...  110 us
    dot_general x1, matrix products, apply_experts(): lax.dot_general(hidden, weights[2, 0], (((1,), (1,)), ((), ())), preferre...  9.35 us
  transfers between devices with their start and end apart: 1, of which 0 were waited for; matrix products, arithmetic and copies ran while one was open for 2% of the time, Pallas kernels for 0%

profile of v6, /device:TPU:6, one launch (start us, length us, event | category | flops | bytes accessed | tf_op | source)
XLA Modules:
  0.0 262.5 jit_solution(1736838912406592165)
XLA Ops:
  6.5 0.0 copy-start
  6.5 0.0 all-gather.2.cloned.1.call-start
  6.5 1.6 pad_maximum_fusion
  8.1 0.0 all-gather.2.cloned.1.call-update
  8.1 0.8 select_reduce_fusion.2
  9.0 0.1 fusion.8
  9.2 1.9 select_reduce_fusion
  11.1 0.0 copy-done
  11.1 1.4 convolution_convert_fusion.1
  12.5 116.0 %all_to_all.10 = bf16[16,1,72,2048]{3,2,1,0:T(8,128)(2,1)} all-to-all(bf16[16,1,72,2048]{3,2,1,0:T(8,128)(2,1)S(1)} %bitcast.34), channel_id=1, replica_groups=mesh['rep'=32,'exp'=16] {'exp'}, dimensions={0} | all-to-all | bytes 9437184 | tf_op jit(solution)/shard_map/all_to_all | solution.py:47
  128.5 0.0 all-gather.2.cloned.1.call-done
  128.5 4.9 %fusion.2 = f32[1152,384]{1,0:T(8,128)S(1)} fusion(bf16[1152,2048]{1,0:T(8,128)(2,1)} %bitcast.35, bf16[3,1,2048,384]{3,2,1,0:T(8,128)(2,1)} %all-gather.2.cloned.1.call-done), kind=kOutput, calls=%fused_computation.12 | convolution fusion | flops 1811939328 | bytes 8060928 | tf_op jit(solution)/shard_map/dot_general | solution.py:12
  133.4 9.4 %convolution_convert_fusion = bf16[1152,2048]{1,0:T(8,128)(2,1)} fusion(bf16[3,1,2048,384]{3,2,1,0:T(8,128)(2,1)} %all-gather.2.cloned.1.call-done, bf16[1152,2048]{1,0:T(8,128)(2,1)} %bitcast.36, f32[1152,384]{1,0:T(8,128)S(1)} %fusion.2), kind=kOutput, calls=%fused_computation | convolution fusion | flops 3628892160 | bytes 14352384 | tf_op jit(solution)/shard_map/dot_general | solution.py:15
  142.7 110.4 %all_to_all.11 = bf16[16,1,72,2048]{3,2,1,0:T(8,128)(2,1)S(1)} all-to-all(bf16[16,1,72,2048]{3,2,1,0:T(8,128)(2,1)} %bitcast.37), channel_id=1, replica_groups=mesh['rep'=32,'exp'=16] {'exp'}, dimensions={0} | all-to-all | bytes 9437184 | tf_op jit(solution)/shard_map/all_to_all | solution.py:48
  253.1 0.9 fusion.6
  254.0 1.7 fusion.1
  (3 shorter events, 0.1 us)
Async XLA Ops:
  6.5 4.6 %copy-start = (bf16[128,2048]{1,0:T(8,128)(2,1)S(1)}, bf16[128,2048]{1,0:T(8,128)(2,1)}, u32[]{:S(2)}) copy-start(bf16[128,2048]{1,0:T(8,128)(2,1)} %param.7) | copy-start | bytes 1572868
  6.5 121.9 %all-gather.2.cloned.1.call-start = ((), (), s32[]{:S(2)}) async-start(), calls=%async_computation.2 | async-start | bytes 4866048 | tf_op jit(solution)/shard_map/all_gather | solution.py:46
Sparse Core Ops, SparseCore 0:
  10.5 93.1 all-gather.1

commit v7 on v6

--- a/solution.py
+++ b/solution.py
@@ -12,6 +12,7 @@
     gate_value = jnp.dot(row_block, weights[0, 0], preferred_element_type=jnp.float32)
     up_value = jnp.dot(row_block, weights[1, 0], preferred_element_type=jnp.float32)
     hidden = (jax.nn.silu(gate_value) * up_value).astype(jnp.bfloat16)
+    hidden = lax.optimization_barrier(hidden)
     result = lax.dot_general(
         hidden, weights[2, 0], (((1,), (1,)), ((), ())), preferred_element_type=jnp.float32
     )

time: 263 us -> 260 us (0.989)
  matrix products: 18.4 us -> 14.9 us
    dot_general x1, matrix products: 9.35 us -> 2.89 us  [apply_experts(): lax.dot_general(hidden, weights[2, 0], (((1,), (1,)), ((), ())), preferre...]
    dot_general x0 -> x1, matrix products: none -> 2.88 us  [apply_experts(): jnp.dot(row_block, weights[1, 0], preferred_element_type=jnp.float32)]
where the time goes in v7:
time: 260 us
  blocking collectives  226 us (87%)
  matrix products  14.9 us (6%)
  between operations  13.5 us (5%)
  other arithmetic  4.37 us (2%)
    all_to_all x1, blocking collectives, on_device(): lax.all_to_all(outgoing, 'exp', split_axis=0, concat_axis=0, tiled=True)  116 us
    all_to_all x1, blocking collectives, on_device(): lax.all_to_all(apply_experts(received, stacked), 'exp', split_axis=0, con...  110 us
  transfers between devices with their start and end apart: 1, of which 0 were waited for; matrix products, arithmetic and copies ran while one was open for 2% of the time, Pallas kernels for 0%

profile of v7, /device:TPU:6, one launch (start us, length us, event | category | flops | bytes accessed | tf_op | source)
XLA Modules:
  0.0 259.8 jit_solution(9751797197174515544)
XLA Ops:
  6.5 0.0 copy-start
  6.5 0.0 all-gather.2.cloned.1.call-start
  6.5 1.6 pad_maximum_fusion
  8.1 0.0 all-gather.2.cloned.1.call-update
  8.1 0.8 select_reduce_fusion.2
  9.0 0.1 fusion.7
  9.2 1.9 select_reduce_fusion
  11.1 0.0 copy-done
  11.1 1.4 convolution_convert_fusion.1
  12.5 116.0 %all_to_all.10 = bf16[16,1,72,2048]{3,2,1,0:T(8,128)(2,1)} all-to-all(bf16[16,1,72,2048]{3,2,1,0:T(8,128)(2,1)S(1)} %bitcast.33), channel_id=1, replica_groups=mesh['rep'=32,'exp'=16] {'exp'}, dimensions={0} | all-to-all | bytes 9437184 | tf_op jit(solution)/shard_map/all_to_all | solution.py:48
  128.5 0.0 all-gather.2.cloned.1.call-done
  128.5 0.0 copy-start.1
  128.5 0.0 copy-start.2
  128.5 5.1 %fusion.2 = f32[1152,384]{1,0:T(8,128)S(1)} fusion(bf16[1152,2048]{1,0:T(8,128)(2,1)} %bitcast.34, bf16[3,1,2048,384]{3,2,1,0:T(8,128)(2,1)} %all-gather.2.cloned.1.call-done), kind=kOutput, calls=%fused_computation.12 | convolution fusion | flops 1811939328 | bytes 8060928 | tf_op jit(solution)/shard_map/dot_general | solution.py:12
  133.6 0.0 copy-done.1
  133.6 0.6 copy-done.2
  134.1 2.9 %fusion = bf16[1152,384]{1,0:T(8,128)(2,1)S(1)} fusion(bf16[1152,2048]{1,0:T(8,128)(2,1)S(1)} %bitcast.35, f32[1152,384]{1,0:T(8,128)S(1)} %fusion.2, bf16[3,1,2048,384]{3,2,1,0:T(8,128)(2,1)S(1)} %copy-done.2), kind=kOutput, calls=%fused_computation.6 | convolution fusion | flops 1814593536 | bytes 8945664 | tf_op jit(solution)/shard_map/dot_general | solution.py:13
  137.0 2.9 %convolution_convert_fusion = bf16[1152,2048]{1,0:T(8,128)(2,1)S(1)} fusion(bf16[1152,384]{1,0:T(8,128)(2,1)S(1)} %fusion, bf16[3,1,2048,384]{3,2,1,0:T(8,128)(2,1)S(1)} %copy-done.2), kind=kOutput, calls=%fused_computation | convolution fusion | flops 1814298624 | bytes 7176192 | tf_op jit(solution)/shard_map/dot_general | solution.py:16
  139.9 110.5 %all_to_all.11 = bf16[16,1,72,2048]{3,2,1,0:T(8,128)(2,1)S(1)} all-to-all(bf16[16,1,72,2048]{3,2,1,0:T(8,128)(2,1)S(1)} %bitcast.36), channel_id=1, replica_groups=mesh['rep'=32,'exp'=16] {'exp'}, dimensions={0} | all-to-all | bytes 9437184 | tf_op jit(solution)/shard_map/all_to_all | solution.py:49
  250.4 0.9 fusion.5
  251.3 1.7 fusion.1
  (3 shorter events, 0.1 us)
Async XLA Ops:
  6.5 4.6 %copy-start = (bf16[128,2048]{1,0:T(8,128)(2,1)S(1)}, bf16[128,2048]{1,0:T(8,128)(2,1)}, u32[]{:S(2)}) copy-start(bf16[128,2048]{1,0:T(8,128)(2,1)} %param.7) | copy-start | bytes 1572868
  6.5 122.0 %all-gather.2.cloned.1.call-start = ((), (), s32[]{:S(2)}) async-start(), calls=%async_computation.2 | async-start | bytes 4866048 | tf_op jit(solution)/shard_map/all_gather | solution.py:47
  128.5 5.1 %copy-start.1 = (bf16[16,1,72,2048]{3,2,1,0:T(8,128)(2,1)S(1)}, bf16[16,1,72,2048]{3,2,1,0:T(8,128)(2,1)}, u32[]{:S(2)}) copy-start(bf16[16,1,72,2048]{3,2,1,0:T(8,128)(2,1)} %all_to_all.10) | copy-start | bytes 14155780
  128.5 5.6 %copy-start.2 = (bf16[3,1,2048,384]{3,2,1,0:T(8,128)(2,1)S(1)}, bf16[3,1,2048,384]{3,2,1,0:T(8,128)(2,1)}, u32[]{:S(2)}) copy-start(bf16[3,1,2048,384]{3,2,1,0:T(8,128)(2,1)} %all-gather.2.cloned.1.call-done) | copy-start | bytes 14155780
Sparse Core Ops, SparseCore 0:
  10.5 93.1 all-gather.1

commit v8 on v7

--- a/solution.py
+++ b/solution.py
@@ -6,15 +6,16 @@
 CAP = 72
 
 
-def apply_experts(received, weights):
+def apply_experts(received, weights, hidden_width):
     sources, local_count, capacity, model_width = received.shape
     row_block = received[:, 0].reshape(-1, model_width)
-    gate_value = jnp.dot(row_block, weights[0, 0], preferred_element_type=jnp.float32)
-    up_value = jnp.dot(row_block, weights[1, 0], preferred_element_type=jnp.float32)
+    both = jnp.dot(row_block, weights[0, :, : 2 * hidden_width], preferred_element_type=jnp.float32)
+    gate_value, up_value = both[:, :hidden_width], both[:, hidden_width:]
     hidden = (jax.nn.silu(gate_value) * up_value).astype(jnp.bfloat16)
     hidden = lax.optimization_barrier(hidden)
     result = lax.dot_general(
-        hidden, weights[2, 0], (((1,), (1,)), ((), ())), preferred_element_type=jnp.float32
+        hidden, weights[0, :, 2 * hidden_width :], (((1,), (1,)), ((), ())),
+        preferred_element_type=jnp.float32,
     )
     results = [result.astype(jnp.bfloat16).reshape(sources, capacity, model_width)]
     return jnp.stack(results, axis=1)
@@ -43,11 +44,11 @@
         scatter, tokens, (((0,), (0,)), ((), ())), preferred_element_type=jnp.float32
     ).astype(jnp.bfloat16)
     outgoing = outgoing.reshape(groups, local_experts, CAP, model_width)
-    stacked = jnp.stack([w_gate, w_up, down_rows])
-    stacked = lax.all_gather(stacked, "rep", axis=2, tiled=True)
+    stacked = jnp.concatenate([w_gate, w_up, down_rows], axis=2)
+    stacked = lax.all_gather(stacked, "rep", axis=1, tiled=True)
     received = lax.all_to_all(outgoing, "exp", split_axis=0, concat_axis=0, tiled=True)
     returned = lax.all_to_all(
-        apply_experts(received, stacked), "exp", split_axis=0, concat_axis=0, tiled=True
+        apply_experts(received, stacked, w_gate.shape[2]), "exp", split_axis=0, concat_axis=0, tiled=True
     )
     returned = returned.reshape(slots_total, model_width)
     combine = jnp.sum(jnp.where(hits, route_weights.T[:, :, None], 0.0), axis=0)

time: 260 us -> 260 us (level)
    dot_general x3 -> x2, matrix products: 10.8 us -> 10.9 us  [the longest x1 6.61 us: apply_experts(): jnp.dot(row_block, weights[0, :, :2 * hidden_width], preferred_element_ty...]
where the time goes in v8:
time: 260 us
  blocking collectives  226 us (87%)
  matrix products  15 us (6%)
  between operations  13.5 us (5%)
  other arithmetic  4.87 us (2%)
    all_to_all x1, blocking collectives, on_device(): lax.all_to_all(outgoing, 'exp', split_axis=0, concat_axis=0, tiled=True)  116 us
    all_to_all x1, blocking collectives, on_device(): lax.all_to_all(apply_experts(received, stacked, w_gate.shape[2]), 'exp',...  110 us
    dot_general x1, matrix products, apply_experts(): jnp.dot(row_block, weights[0, :, :2 * hidden_width], preferred_element_ty...  6.61 us
  transfers between devices with their start and end apart: 1, of which 0 were waited for; matrix products, arithmetic and copies ran while one was open for 2% of the time, Pallas kernels for 0%

profile of v8, /device:TPU:6, one launch (start us, length us, event | category | flops | bytes accessed | tf_op | source)
XLA Modules:
  0.0 259.8 jit_solution(9743765526536133137)
XLA Ops:
  6.5 0.0 copy-start
  6.5 0.0 all-gather.2.cloned.1.call-start
  6.5 1.6 pad_maximum_fusion
  8.1 0.0 all-gather.2.cloned.1.call-update
  8.1 0.8 select_reduce_fusion.2
  9.0 0.1 fusion.7
  9.1 1.9 select_reduce_fusion
  11.1 0.0 copy-done
  11.1 1.4 convolution_convert_fusion.1
  12.5 116.0 %all_to_all.10 = bf16[16,1,72,2048]{3,2,1,0:T(8,128)(2,1)} all-to-all(bf16[16,1,72,2048]{3,2,1,0:T(8,128)(2,1)S(1)} %bitcast.26), channel_id=1, replica_groups=mesh['rep'=32,'exp'=16] {'exp'}, dimensions={0} | all-to-all | bytes 9437184 | tf_op jit(solution)/shard_map/all_to_all | solution.py:49
  128.5 0.0 all-gather.2.cloned.1.call-done
  128.5 6.6 %fusion = f32[1152,768]{1,0:T(8,128)S(1)} fusion(bf16[1152,2048]{1,0:T(8,128)(2,1)} %bitcast.27, bf16[1,2048,1152]{2,1,0:T(8,128)(2,1)} %all-gather.2.cloned.1.call-done), kind=kOutput, calls=%fused_computation.6 | convolution fusion | flops 3623878656 | bytes 11403264 | tf_op jit(solution)/shard_map/dot_general | solution.py:12
  135.1 0.5 fusion.2
  135.6 4.3 %convolution_convert_fusion = bf16[1152,2048]{1,0:T(8,128)(2,1)S(1)} fusion(bf16[1152,384]{1,0:T(8,128)(2,1)S(1)} %fusion.2, bf16[1,2048,1152]{2,1,0:T(8,128)(2,1)} %all-gather.2.cloned.1.call-done), kind=kOutput, calls=%fused_computation | convolution fusion | flops 1814298624 | bytes 7176192 | tf_op jit(solution)/shard_map/dot_general | solution.py:16
  139.9 110.5 %all_to_all.11 = bf16[16,1,72,2048]{3,2,1,0:T(8,128)(2,1)S(1)} all-to-all(bf16[16,1,72,2048]{3,2,1,0:T(8,128)(2,1)S(1)} %bitcast.28), channel_id=1, replica_groups=mesh['rep'=32,'exp'=16] {'exp'}, dimensions={0} | all-to-all | bytes 9437184 | tf_op jit(solution)/shard_map/all_to_all | solution.py:50
  250.4 0.9 fusion.5
  251.3 1.7 fusion.1
  (3 shorter events, 0.1 us)
Async XLA Ops:
  6.5 4.5 %copy-start = (bf16[128,2048]{1,0:T(8,128)(2,1)S(1)}, bf16[128,2048]{1,0:T(8,128)(2,1)}, u32[]{:S(2)}) copy-start(bf16[128,2048]{1,0:T(8,128)(2,1)} %param.7) | copy-start | bytes 1572868
  6.5 121.9 %all-gather.2.cloned.1.call-start = ((), (), s32[]{:S(2)}) async-start(), calls=%async_computation.2 | async-start | bytes 4866048 | tf_op jit(solution)/shard_map/all_gather | solution.py:48
Sparse Core Ops, SparseCore 0:
  10.5 93.1 all-gather.1

commit v9 on v6

--- a/solution.py
+++ b/solution.py
@@ -11,6 +11,7 @@
     row_block = received[:, 0].reshape(-1, model_width)
     gate_value = jnp.dot(row_block, weights[0, 0], preferred_element_type=jnp.float32)
     up_value = jnp.dot(row_block, weights[1, 0], preferred_element_type=jnp.float32)
+    gate_value, up_value = lax.optimization_barrier((gate_value, up_value))
     hidden = (jax.nn.silu(gate_value) * up_value).astype(jnp.bfloat16)
     result = lax.dot_general(
         hidden, weights[2, 0], (((1,), (1,)), ((), ())), preferred_element_type=jnp.float32

time: 263 us -> 260 us (0.989)
  matrix products: 18.4 us -> 14.7 us
    dot_general x1, matrix products: 9.35 us -> 2.92 us  [apply_experts(): lax.dot_general(hidden, weights[2, 0], (((1,), (1,)), ((), ())), preferre...]
    dot_general x0 -> x1, matrix products: none -> 5.05 us  [apply_experts(): jnp.dot(row_block, weights[1, 0], preferred_element_type=jnp.float32)]
where the time goes in v9:
time: 260 us
  blocking collectives  226 us (87%)
  matrix products  14.7 us (6%)
  between operations  13.5 us (5%)
  other arithmetic  4.37 us (2%)
    all_to_all x1, blocking collectives, on_device(): lax.all_to_all(outgoing, 'exp', split_axis=0, concat_axis=0, tiled=True)  116 us
    all_to_all x1, blocking collectives, on_device(): lax.all_to_all(apply_experts(received, stacked), 'exp', split_axis=0, con...  110 us
  transfers between devices with their start and end apart: 1, of which 0 were waited for; matrix products, arithmetic and copies ran while one was open for 2% of the time, Pallas kernels for 0%

profile of v9, /device:TPU:6, one launch (start us, length us, event | category | flops | bytes accessed | tf_op | source)
XLA Modules:
  0.0 259.6 jit_solution(5752277103701781787)
XLA Ops:
  6.5 0.0 copy-start
  6.5 0.0 all-gather.2.cloned.1.call-start
  6.5 1.6 pad_maximum_fusion
  8.1 0.0 all-gather.2.cloned.1.call-update
  8.1 0.8 select_reduce_fusion.2
  9.0 0.1 fusion.8
  9.2 1.9 select_reduce_fusion
  11.1 0.0 copy-done
  11.1 1.4 convolution_convert_fusion.1
  12.5 116.0 %all_to_all.10 = bf16[16,1,72,2048]{3,2,1,0:T(8,128)(2,1)} all-to-all(bf16[16,1,72,2048]{3,2,1,0:T(8,128)(2,1)S(1)} %bitcast.32), channel_id=1, replica_groups=mesh['rep'=32,'exp'=16] {'exp'}, dimensions={0} | all-to-all | bytes 9437184 | tf_op jit(solution)/shard_map/all_to_all | solution.py:48
  128.5 0.0 all-gather.2.cloned.1.call-done
  128.5 0.0 copy-start.1
  128.5 0.0 copy-start.2
  128.5 5.1 %fusion.1 = f32[1152,384]{1,0:T(8,128)S(1)} fusion(bf16[1152,2048]{1,0:T(8,128)(2,1)} %bitcast.33, bf16[3,1,2048,384]{3,2,1,0:T(8,128)(2,1)} %all-gather.2.cloned.1.call-done), kind=kOutput, calls=%fused_computation.10 | convolution fusion | flops 1811939328 | bytes 8060928 | tf_op jit(solution)/shard_map/dot_general | solution.py:13
  133.6 0.0 copy-done.1
  133.6 0.6 copy-done.2
  134.1 2.6 %fusion.2 = f32[1152,384]{1,0:T(8,128)S(1)} fusion(bf16[1152,2048]{1,0:T(8,128)(2,1)S(1)} %bitcast.34, bf16[3,1,2048,384]{3,2,1,0:T(8,128)(2,1)S(1)} %copy-done.2), kind=kOutput, calls=%fused_computation.12 | convolution fusion | flops 1811939328 | bytes 8060928 | tf_op jit(solution)/shard_map/dot_general | solution.py:12
  136.7 2.9 %convolution_convert_fusion = bf16[1152,2048]{1,0:T(8,128)(2,1)S(1)} fusion(bf16[3,1,2048,384]{3,2,1,0:T(8,128)(2,1)S(1)} %copy-done.2, f32[1152,384]{1,0:T(8,128)S(1)} %fusion.1, f32[1152,384]{1,0:T(8,128)S(1)} %fusion.2), kind=kOutput, calls=%fused_computation | convolution fusion | flops 1816952832 | bytes 9830400 | tf_op jit(solution)/shard_map/dot_general | solution.py:16
  139.7 110.5 %all_to_all.11 = bf16[16,1,72,2048]{3,2,1,0:T(8,128)(2,1)S(1)} all-to-all(bf16[16,1,72,2048]{3,2,1,0:T(8,128)(2,1)S(1)} %bitcast.35), channel_id=1, replica_groups=mesh['rep'=32,'exp'=16] {'exp'}, dimensions={0} | all-to-all | bytes 9437184 | tf_op jit(solution)/shard_map/all_to_all | solution.py:49
  250.2 0.9 fusion.6
  251.0 1.7 fusion
  (3 shorter events, 0.1 us)
Async XLA Ops:
  6.5 4.6 %copy-start = (bf16[128,2048]{1,0:T(8,128)(2,1)S(1)}, bf16[128,2048]{1,0:T(8,128)(2,1)}, u32[]{:S(2)}) copy-start(bf16[128,2048]{1,0:T(8,128)(2,1)} %param.7) | copy-start | bytes 1572868
  6.5 122.0 %all-gather.2.cloned.1.call-start = ((), (), s32[]{:S(2)}) async-start(), calls=%async_computation.2 | async-start | bytes 4866048 | tf_op jit(solution)/shard_map/all_gather | solution.py:47
  128.5 5.1 %copy-start.1 = (bf16[16,1,72,2048]{3,2,1,0:T(8,128)(2,1)S(1)}, bf16[16,1,72,2048]{3,2,1,0:T(8,128)(2,1)}, u32[]{:S(2)}) copy-start(bf16[16,1,72,2048]{3,2,1,0:T(8,128)(2,1)} %all_to_all.10) | copy-start | bytes 14155780
  128.5 5.6 %copy-start.2 = (bf16[3,1,2048,384]{3,2,1,0:T(8,128)(2,1)S(1)}, bf16[3,1,2048,384]{3,2,1,0:T(8,128)(2,1)}, u32[]{:S(2)}) copy-start(bf16[3,1,2048,384]{3,2,1,0:T(8,128)(2,1)} %all-gather.2.cloned.1.call-done) | copy-start | bytes 14155780
Sparse Core Ops, SparseCore 0:
  10.5 93.1 all-gather.1

commit v10 on v6

--- a/solution.py
+++ b/solution.py
@@ -1,21 +1,38 @@
 import jax
 import jax.numpy as jnp
 from jax import lax
+from jax.experimental import pallas as pl
 from jax.sharding import PartitionSpec as P
 
 CAP = 72
 
 
+def expert_block(x_ref, gate_ref, up_ref, down_ref, out_ref):
+    x = x_ref[...]
+    gate_value = jnp.dot(x, gate_ref[...], preferred_element_type=jnp.float32)
+    up_value = jnp.dot(x, up_ref[...], preferred_element_type=jnp.float32)
+    hidden = (gate_value / (1.0 + jnp.exp(-gate_value)) * up_value).astype(jnp.bfloat16)
+    result = lax.dot_general(
+        hidden, down_ref[...], (((1,), (1,)), ((), ())), preferred_element_type=jnp.float32
+    )
+    out_ref[...] = result.astype(out_ref.dtype)
+
+
 def apply_experts(received, weights):
     sources, local_count, capacity, model_width = received.shape
+    hidden_width = weights.shape[-1]
     row_block = received[:, 0].reshape(-1, model_width)
-    gate_value = jnp.dot(row_block, weights[0, 0], preferred_element_type=jnp.float32)
-    up_value = jnp.dot(row_block, weights[1, 0], preferred_element_type=jnp.float32)
-    hidden = (jax.nn.silu(gate_value) * up_value).astype(jnp.bfloat16)
-    result = lax.dot_general(
-        hidden, weights[2, 0], (((1,), (1,)), ((), ())), preferred_element_type=jnp.float32
-    )
-    results = [result.astype(jnp.bfloat16).reshape(sources, capacity, model_width)]
+    rows = row_block.shape[0]
+    block = 128
+    weight_spec = pl.BlockSpec((model_width, hidden_width), lambda i: (0, 0))
+    result = pl.pallas_call(
+        expert_block,
+        grid=(rows // block,),
+        in_specs=[pl.BlockSpec((block, model_width), lambda i: (i, 0)), weight_spec, weight_spec, weight_spec],
+        out_specs=pl.BlockSpec((block, model_width), lambda i: (i, 0)),
+        out_shape=jax.ShapeDtypeStruct((rows, model_width), jnp.bfloat16),
+    )(row_block, weights[0, 0], weights[1, 0], weights[2, 0])
+    results = [result.reshape(sources, capacity, model_width)]
     return jnp.stack(results, axis=1)
 
 

time: 263 us -> 284 us (1.080)
  waiting for transfers between devices: 0.02 us -> 103 us
  blocking collectives: 226 us -> 128 us
  Pallas kernels: 0 us -> 14.7 us
  matrix products: 18.4 us -> 6.36 us
  starting transfers between devices: 0.01 us -> 9.06 us
  local copies, waits for them, and re-layouts: 0.01 us -> 4.65 us
    all_to_all x1 -> x0, blocking collectives: 116 us -> none  [on_device(): lax.all_to_all(outgoing, 'exp', split_axis=0, concat_axis=0, tiled=True)]
    all_gather x1, waiting for transfers between devices: 0.01 us -> 67.4 us  [on_device(): stacked = lax.all_gather(stacked, 'rep', axis=2, tiled=True)]
    all_to_all x0 -> x1, waiting for transfers between devices: none -> 35.9 us  [on_device(): lax.all_to_all(outgoing, 'exp', split_axis=0, concat_axis=0, tiled=True)]
    all_to_all x1, blocking collectives: 110 us -> 128 us  [on_device(): lax.all_to_all(apply_experts(received, stacked), 'exp', split_axis=0, con...]
    pallas_call x0 -> x1, Pallas kernels: none -> 14.7 us  [apply_experts(): pl.pallas_call(expert_block, grid=(rows // block,), in_specs=[pl.BlockSpe...]
    dot_general x2 -> x0, matrix products: 14.3 us -> none  [the longest x1 9.35 us: apply_experts(): lax.dot_general(hidden, weights[2, 0], (((1,), (1,)), ((), ())), preferre...]
    all_to_all x0 -> x1, starting transfers between devices: none -> 9.06 us  [on_device(): lax.all_to_all(outgoing, 'exp', split_axis=0, concat_axis=0, tiled=True)]
    squeeze x0 -> x1, local copies, waits for them, and re-layouts: none -> 4.64 us  [apply_experts(): weights[2, 0]]
  transfers between devices with their start and end apart: 1 -> 2, of which waited for: 0 -> 2; matrix products, arithmetic and copies ran while one was open for 2% -> 4% of each run, Pallas kernels for 0% -> 0%
where the time goes in v10:
time: 284 us
  blocking collectives  128 us (45%)
  waiting for transfers between devices  103 us (36%)
  Pallas kernels  14.7 us (5%)
  between operations  13.4 us (5%)
  starting transfers between devices  9.06 us (3%)
  matrix products  6.36 us (2%)
  local copies, waits for them, and re-layouts  4.65 us (2%)
  other arithmetic  4.35 us (2%)
    all_to_all x1, blocking collectives, on_device(): lax.all_to_all(apply_experts(received, stacked), 'exp', split_axis=0, con...  128 us
    all_gather x1, waiting for transfers between devices, on_device(): stacked = lax.all_gather(stacked, 'rep', axis=2, tiled=True)  67.4 us
    all_to_all x1, waiting for transfers between devices, on_device(): lax.all_to_all(outgoing, 'exp', split_axis=0, concat_axis=0, tiled=True)  35.9 us
    pallas_call x1, Pallas kernels, apply_experts(): pl.pallas_call(expert_block, grid=(rows // block,), in_specs=[pl.BlockSpe...  14.7 us
    all_to_all x1, starting transfers between devices, on_device(): lax.all_to_all(outgoing, 'exp', split_axis=0, concat_axis=0, tiled=True)  9.06 us
  transfers between devices with their start and end apart: 2, of which 2 were waited for; matrix products, arithmetic and copies ran while one was open for 4% of the time, Pallas kernels for 0%

profile of v10, /device:TPU:6, one launch (start us, length us, event | category | flops | bytes accessed | tf_op | source)
XLA Modules:
  0.0 283.7 jit_solution(5543560343803959875)
XLA Ops:
  6.5 0.0 copy-start
  6.5 0.0 all-gather.2.cloned.1.call-start
  6.5 1.6 pad_maximum_fusion
  8.1 0.0 all-gather.2.cloned.1.call-update
  8.1 0.8 select_reduce_fusion.2
  9.0 0.1 fusion.5
  9.2 1.9 select_reduce_fusion
  11.1 0.0 copy-done
  11.1 3.6 %convolution_convert_fusion = bf16[1152,2048]{1,0:T(8,128)(2,1)} fusion(bf16[128,2048]{1,0:T(8,128)(2,1)S(1)} %copy-done, bf16[128,1152]{1,0:T(8,128)(2,1)S(1)} %get-tuple-element.6), kind=kOutput, calls=%fused_computation | convolution fusion | flops 606339072 | bytes 5537792 | tf_op jit(solution)/shard_map/dot_general | solution.py:58
  14.7 9.1 %all-to-all-start = ((bf16[16,1,72,2048]{3,2,1,0:T(8,128)(2,1)}), bf16[16,1,72,2048]{3,2,1,0:T(8,128)(2,1)}, u32[]{:S(2)}, u32[]{:S(2)}) async-start(bf16[16,1,72,2048]{3,2,1,0:T(8,128)(2,1)} %bitcast.27), calls=%async_computation | async-start | bytes 9437184 | tf_op jit(solution)/shard_map/all_to_all | solution.py:64
  23.8 67.4 %all-gather.2.cloned.1.call-done = bf16[3,1,2048,384]{3,2,1,0:T(8,128)(2,1)} async-done(((bf16[3,1,64,384]{3,2,1,0:T(8,128)(2,1)}), bf16[3,1,2048,384]{3,2,1,0:T(8,128)(2,1)}) %all-gather.2.cloned.1.call-update) | async-done | bytes 4718608 | tf_op jit(solution)/shard_map/all_gather | solution.py:63
  91.2 4.6 %slice_bitcast_fusion = (bf16[2048,384]{1,0:T(8,128)(2,1)}, bf16[2048,384]{1,0:T(8,128)(2,1)}, bf16[2048,384]{1,0:T(8,128)(2,1)}) fusion(bf16[3,1,2048,384]{3,2,1,0:T(8,128)(2,1)} %all-gather.2.cloned.1.call-done), kind=kLoop, calls=%fused_computation.6 | loop fusion | bytes 9437184 | tf_op jit(solution)/shard_map/squeeze | solution.py:34
  95.9 35.9 %all-to-all-done = bf16[16,1,72,2048]{3,2,1,0:T(8,128)(2,1)} async-done(((bf16[16,1,72,2048]{3,2,1,0:T(8,128)(2,1)}), bf16[16,1,72,2048]{3,2,1,0:T(8,128)(2,1)}, u32[]{:S(2)}, u32[]{:S(2)}) %all-to-all-start) | async-done | bytes 4718624 | tf_op jit(solution)/shard_map/all_to_all | solution.py:64
  131.8 14.7 %shard_map.73 = bf16[1152,2048]{1,0:T(8,128)(2,1)} custom-call(bf16[1152,2048]{1,0:T(8,128)(2,1)} %bitcast.4.x_ref, bf16[2048,384]{1,0:T(8,128)(2,1)} %get-tuple-element.9.gate_ref, bf16[2048,384]{1,0:T(8,128)(2,1)} %get-tuple-element.8.up_ref, bf16[2048,384]{1,0:T(8,128)(2,1)} %get-tuple-element.7.down_ref), custom_call_target="tpu_custom_call" | custom-call | tf_op jit(solution)/shard_map/pallas_call | solution.py:28
  146.5 127.8 %all_to_all.10 = bf16[16,1,72,2048]{3,2,1,0:T(8,128)(2,1)S(1)} all-to-all(bf16[16,1,72,2048]{3,2,1,0:T(8,128)(2,1)} %bitcast.28), channel_id=1, replica_groups=mesh['rep'=32,'exp'=16] {'exp'}, dimensions={0} | all-to-all | bytes 9437184 | tf_op jit(solution)/shard_map/all_to_all | solution.py:65
  274.3 0.9 fusion.3
  275.2 1.7 fusion
  (3 shorter events, 0.1 us)
Async XLA Ops:
  6.5 4.6 %copy-start = (bf16[128,2048]{1,0:T(8,128)(2,1)S(1)}, bf16[128,2048]{1,0:T(8,128)(2,1)}, u32[]{:S(2)}) copy-start(bf16[128,2048]{1,0:T(8,128)(2,1)} %param.7) | copy-start | bytes 1572868
  6.5 84.7 %all-gather.2.cloned.1.call-start = ((), (), s32[]{:S(2)}) async-start(), calls=%async_computation.2 | async-start | bytes 4866048 | tf_op jit(solution)/shard_map/all_gather | solution.py:63
  14.7 117.1 %all-to-all-start = ((bf16[16,1,72,2048]{3,2,1,0:T(8,128)(2,1)}), bf16[16,1,72,2048]{3,2,1,0:T(8,128)(2,1)}, u32[]{:S(2)}, u32[]{:S(2)}) async-start(bf16[16,1,72,2048]{3,2,1,0:T(8,128)(2,1)} %bitcast.27), calls=%async_computation | async-start | bytes 9437184 | tf_op jit(solution)/shard_map/all_to_all | solution.py:64
Sparse Core Ops, SparseCore 0:
  10.5 80.6 all-gather.1

commit v11 on v10

--- a/solution.py
+++ b/solution.py
@@ -23,15 +23,16 @@
     hidden_width = weights.shape[-1]
     row_block = received[:, 0].reshape(-1, model_width)
     rows = row_block.shape[0]
-    block = 128
-    weight_spec = pl.BlockSpec((model_width, hidden_width), lambda i: (0, 0))
+    block = 384
+    def pick(k):
+        return pl.BlockSpec((None, None, model_width, hidden_width), lambda i: (k, 0, 0, 0))
     result = pl.pallas_call(
         expert_block,
         grid=(rows // block,),
-        in_specs=[pl.BlockSpec((block, model_width), lambda i: (i, 0)), weight_spec, weight_spec, weight_spec],
+        in_specs=[pl.BlockSpec((block, model_width), lambda i: (i, 0)), pick(0), pick(1), pick(2)],
         out_specs=pl.BlockSpec((block, model_width), lambda i: (i, 0)),
         out_shape=jax.ShapeDtypeStruct((rows, model_width), jnp.bfloat16),
-    )(row_block, weights[0, 0], weights[1, 0], weights[2, 0])
+    )(row_block, weights, weights, weights)
     results = [result.reshape(sources, capacity, model_width)]
     return jnp.stack(results, axis=1)
 

time: 284 us -> 261 us (0.919)
  waiting for transfers between devices: 103 us -> 0.02 us
  blocking collectives: 128 us -> 226 us
  starting transfers between devices: 9.06 us -> 0.01 us
  local copies, waits for them, and re-layouts: 4.65 us -> 0.01 us
    all_to_all x0 -> x1, blocking collectives: none -> 116 us  [on_device(): lax.all_to_all(outgoing, 'exp', split_axis=0, concat_axis=0, tiled=True)]
    all_gather x1, waiting for transfers between devices: 67.4 us -> 0.01 us  [on_device(): stacked = lax.all_gather(stacked, 'rep', axis=2, tiled=True)]
    all_to_all x1 -> x0, waiting for transfers between devices: 35.9 us -> none  [on_device(): lax.all_to_all(outgoing, 'exp', split_axis=0, concat_axis=0, tiled=True)]
    all_to_all x1, blocking collectives: 128 us -> 110 us  [on_device(): lax.all_to_all(apply_experts(received, stacked), 'exp', split_axis=0, con...]
    all_to_all x1 -> x0, starting transfers between devices: 9.06 us -> none  [on_device(): lax.all_to_all(outgoing, 'exp', split_axis=0, concat_axis=0, tiled=True)]
    squeeze x1 -> x0, local copies, waits for them, and re-layouts: 4.64 us -> none  [apply_experts(): weights[2, 0]]
  transfers between devices with their start and end apart: 2 -> 1, of which waited for: 2 -> 0; matrix products, arithmetic and copies ran while one was open for 4% -> 2% of each run, Pallas kernels for 0% -> 0%
where the time goes in v11:
time: 261 us; the launch traced here: 260 us
  blocking collectives  226 us (87%)
  between operations  13.4 us (5%)
  Pallas kernels  12 us (5%)
  other arithmetic  4.35 us (2%)
  matrix products  4.11 us (2%)
    all_to_all x1, blocking collectives, on_device(): lax.all_to_all(outgoing, 'exp', split_axis=0, concat_axis=0, tiled=True)  116 us
    all_to_all x1, blocking collectives, on_device(): lax.all_to_all(apply_experts(received, stacked), 'exp', split_axis=0, con...  110 us
    pallas_call x1, Pallas kernels, apply_experts(): pl.pallas_call(expert_block, grid=(rows // block,), in_specs=[pl.BlockSpe...  12 us
  transfers between devices with their start and end apart: 1, of which 0 were waited for; matrix products, arithmetic and copies ran while one was open for 2% of the time, Pallas kernels for 0%

profile of v11, /device:TPU:6, one launch (start us, length us, event | category | flops | bytes accessed | tf_op | source)
XLA Modules:
  0.0 260.3 jit_solution(17487084731642608206)
XLA Ops:
  6.5 0.0 copy-start
  6.5 0.0 all-gather.2.cloned.1.call-start
  6.5 1.6 pad_maximum_fusion
  8.1 0.0 all-gather.2.cloned.1.call-update
  8.1 0.8 select_reduce_fusion.2
  9.0 0.1 fusion.5
  9.2 1.9 select_reduce_fusion
  11.1 0.0 copy-done
  11.1 1.4 convolution_convert_fusion
  12.5 116.0 %all_to_all.10 = bf16[16,1,72,2048]{3,2,1,0:T(8,128)(2,1)} all-to-all(bf16[16,1,72,2048]{3,2,1,0:T(8,128)(2,1)S(1)} %bitcast.21), channel_id=1, replica_groups=mesh['rep'=32,'exp'=16] {'exp'}, dimensions={0} | all-to-all | bytes 9437184 | tf_op jit(solution)/shard_map/all_to_all | solution.py:65
  128.5 0.0 all-gather.2.cloned.1.call-done.gate_ref.up_ref.down_ref
  128.5 12.0 %shard_map.73 = bf16[1152,2048]{1,0:T(8,128)(2,1)} custom-call(bf16[1152,2048]{1,0:T(8,128)(2,1)} %bitcast.22, bf16[3,1,2048,384]{3,2,1,0:T(8,128)(2,1)} %all-gather.2.cloned.1.call-done.gate_ref.up_ref.down_ref, bf16[3,1,2048,384]{3,2,1,0:T(8,128)(2,1)} %all-gather.2.cloned.1.call-done.gate_ref.up_ref.down_ref, ...), custom_call_target="tpu_custom_call" | custom-call | tf_op jit(solution)/shard_map/pallas_call | solution.py:29
  140.5 110.4 %all_to_all.11 = bf16[16,1,72,2048]{3,2,1,0:T(8,128)(2,1)S(1)} all-to-all(bf16[16,1,72,2048]{3,2,1,0:T(8,128)(2,1)} %bitcast.23), channel_id=1, replica_groups=mesh['rep'=32,'exp'=16] {'exp'}, dimensions={0} | all-to-all | bytes 9437184 | tf_op jit(solution)/shard_map/all_to_all | solution.py:66
  250.9 0.9 fusion.3
  251.8 1.7 fusion
  (3 shorter events, 0.1 us)
Async XLA Ops:
  6.5 4.6 %copy-start = (bf16[128,2048]{1,0:T(8,128)(2,1)S(1)}, bf16[128,2048]{1,0:T(8,128)(2,1)}, u32[]{:S(2)}) copy-start(bf16[128,2048]{1,0:T(8,128)(2,1)} %param.7) | copy-start | bytes 1572868
  6.5 121.9 %all-gather.2.cloned.1.call-start = ((), (), s32[]{:S(2)}) async-start(), calls=%async_computation.2 | async-start | bytes 4866048 | tf_op jit(solution)/shard_map/all_gather | solution.py:64
Sparse Core Ops, SparseCore 0:
  10.5 93.1 all-gather.1

commit v12 on v11

--- a/solution.py
+++ b/solution.py
@@ -23,7 +23,7 @@
     hidden_width = weights.shape[-1]
     row_block = received[:, 0].reshape(-1, model_width)
     rows = row_block.shape[0]
-    block = 384
+    block = 576
     def pick(k):
         return pl.BlockSpec((None, None, model_width, hidden_width), lambda i: (k, 0, 0, 0))
     result = pl.pallas_call(

time: 261 us -> 261 us (level)
  no operation moved by 1% of the time
where the time goes in v12:
time: 261 us
  blocking collectives  226 us (87%)
  between operations  13.4 us (5%)
  Pallas kernels  12.2 us (5%)
  other arithmetic  4.35 us (2%)
  matrix products  4.11 us (2%)
    all_to_all x1, blocking collectives, on_device(): lax.all_to_all(outgoing, 'exp', split_axis=0, concat_axis=0, tiled=True)  116 us
    all_to_all x1, blocking collectives, on_device(): lax.all_to_all(apply_experts(received, stacked), 'exp', split_axis=0, con...  110 us
    pallas_call x1, Pallas kernels, apply_experts(): pl.pallas_call(expert_block, grid=(rows // block,), in_specs=[pl.BlockSpe...  12.2 us
  transfers between devices with their start and end apart: 1, of which 0 were waited for; matrix products, arithmetic and copies ran while one was open for 2% of the time, Pallas kernels for 0%

profile of v12, /device:TPU:6, one launch (start us, length us, event | category | flops | bytes accessed | tf_op | source)
XLA Modules:
  0.0 260.5 jit_solution(465729338079987669)
XLA Ops:
  6.5 0.0 copy-start
  6.5 0.0 all-gather.2.cloned.1.call-start
  6.5 1.6 pad_maximum_fusion
  8.1 0.0 all-gather.2.cloned.1.call-update
  8.1 0.8 select_reduce_fusion.2
  9.0 0.1 fusion.5
  9.2 1.9 select_reduce_fusion
  11.1 0.0 copy-done
  11.1 1.4 convolution_convert_fusion
  12.5 116.0 %all_to_all.10 = bf16[16,1,72,2048]{3,2,1,0:T(8,128)(2,1)} all-to-all(bf16[16,1,72,2048]{3,2,1,0:T(8,128)(2,1)S(1)} %bitcast.21), channel_id=1, replica_groups=mesh['rep'=32,'exp'=16] {'exp'}, dimensions={0} | all-to-all | bytes 9437184 | tf_op jit(solution)/shard_map/all_to_all | solution.py:65
  128.5 0.0 all-gather.2.cloned.1.call-done.gate_ref.up_ref.down_ref
  128.5 12.2 %shard_map.73 = bf16[1152,2048]{1,0:T(8,128)(2,1)} custom-call(bf16[1152,2048]{1,0:T(8,128)(2,1)} %bitcast.22, bf16[3,1,2048,384]{3,2,1,0:T(8,128)(2,1)} %all-gather.2.cloned.1.call-done.gate_ref.up_ref.down_ref, bf16[3,1,2048,384]{3,2,1,0:T(8,128)(2,1)} %all-gather.2.cloned.1.call-done.gate_ref.up_ref.down_ref, ...), custom_call_target="tpu_custom_call" | custom-call | tf_op jit(solution)/shard_map/pallas_call | solution.py:29
  140.7 110.4 %all_to_all.11 = bf16[16,1,72,2048]{3,2,1,0:T(8,128)(2,1)S(1)} all-to-all(bf16[16,1,72,2048]{3,2,1,0:T(8,128)(2,1)} %bitcast.23), channel_id=1, replica_groups=mesh['rep'=32,'exp'=16] {'exp'}, dimensions={0} | all-to-all | bytes 9437184 | tf_op jit(solution)/shard_map/all_to_all | solution.py:66
  251.1 0.9 fusion.3
  252.0 1.7 fusion
  (3 shorter events, 0.1 us)
Async XLA Ops:
  6.5 4.6 %copy-start = (bf16[128,2048]{1,0:T(8,128)(2,1)S(1)}, bf16[128,2048]{1,0:T(8,128)(2,1)}, u32[]{:S(2)}) copy-start(bf16[128,2048]{1,0:T(8,128)(2,1)} %param.7) | copy-start | bytes 1572868
  6.5 121.9 %all-gather.2.cloned.1.call-start = ((), (), s32[]{:S(2)}) async-start(), calls=%async_computation.2 | async-start | bytes 4866048 | tf_op jit(solution)/shard_map/all_gather | solution.py:64
Sparse Core Ops, SparseCore 0:
  10.5 93.1 all-gather.1

commit v13 on v11

--- a/solution.py
+++ b/solution.py
@@ -7,10 +7,11 @@
 CAP = 72
 
 
-def expert_block(x_ref, gate_ref, up_ref, down_ref, out_ref):
+def expert_block(x_ref, gate_up_ref, down_ref, out_ref):
     x = x_ref[...]
-    gate_value = jnp.dot(x, gate_ref[...], preferred_element_type=jnp.float32)
-    up_value = jnp.dot(x, up_ref[...], preferred_element_type=jnp.float32)
+    hidden_width = down_ref.shape[-1]
+    both = jnp.dot(x, gate_up_ref[...], preferred_element_type=jnp.float32)
+    gate_value, up_value = both[:, :hidden_width], both[:, hidden_width:]
     hidden = (gate_value / (1.0 + jnp.exp(-gate_value)) * up_value).astype(jnp.bfloat16)
     result = lax.dot_general(
         hidden, down_ref[...], (((1,), (1,)), ((), ())), preferred_element_type=jnp.float32
@@ -18,21 +19,22 @@
     out_ref[...] = result.astype(out_ref.dtype)
 
 
-def apply_experts(received, weights):
+def apply_experts(received, weights, hidden_width):
     sources, local_count, capacity, model_width = received.shape
-    hidden_width = weights.shape[-1]
     row_block = received[:, 0].reshape(-1, model_width)
     rows = row_block.shape[0]
     block = 384
-    def pick(k):
-        return pl.BlockSpec((None, None, model_width, hidden_width), lambda i: (k, 0, 0, 0))
     result = pl.pallas_call(
         expert_block,
         grid=(rows // block,),
-        in_specs=[pl.BlockSpec((block, model_width), lambda i: (i, 0)), pick(0), pick(1), pick(2)],
+        in_specs=[
+            pl.BlockSpec((block, model_width), lambda i: (i, 0)),
+            pl.BlockSpec((None, model_width, 2 * hidden_width), lambda i: (0, 0, 0)),
+            pl.BlockSpec((None, model_width, hidden_width), lambda i: (0, 0, 2)),
+        ],
         out_specs=pl.BlockSpec((block, model_width), lambda i: (i, 0)),
         out_shape=jax.ShapeDtypeStruct((rows, model_width), jnp.bfloat16),
-    )(row_block, weights, weights, weights)
+    )(row_block, weights, weights)
     results = [result.reshape(sources, capacity, model_width)]
     return jnp.stack(results, axis=1)
 
@@ -60,11 +62,11 @@
         scatter, tokens, (((0,), (0,)), ((), ())), preferred_element_type=jnp.float32
     ).astype(jnp.bfloat16)
     outgoing = outgoing.reshape(groups, local_experts, CAP, model_width)
-    stacked = jnp.stack([w_gate, w_up, down_rows])
-    stacked = lax.all_gather(stacked, "rep", axis=2, tiled=True)
+    stacked = jnp.concatenate([w_gate, w_up, down_rows], axis=2)
+    stacked = lax.all_gather(stacked, "rep", axis=1, tiled=True)
     received = lax.all_to_all(outgoing, "exp", split_axis=0, concat_axis=0, tiled=True)
     returned = lax.all_to_all(
-        apply_experts(received, stacked), "exp", split_axis=0, concat_axis=0, tiled=True
+        apply_experts(received, stacked, w_gate.shape[2]), "exp", split_axis=0, concat_axis=0, tiled=True
     )
     returned = returned.reshape(slots_total, model_width)
     combine = jnp.sum(jnp.where(hits, route_weights.T[:, :, None], 0.0), axis=0)

time: 261 us -> 262 us (level)
  no operation moved by 1% of the time
where the time goes in v13:
time: 262 us
  blocking collectives  226 us (86%)
  between operations  13.4 us (5%)
  Pallas kernels  13.2 us (5%)
  other arithmetic  4.34 us (2%)
  matrix products  4.12 us (2%)
    all_to_all x1, blocking collectives, on_device(): lax.all_to_all(outgoing, 'exp', split_axis=0, concat_axis=0, tiled=True)  116 us
    all_to_all x1, blocking collectives, on_device(): lax.all_to_all(apply_experts(received, stacked, w_gate.shape[2]), 'exp',...  110 us
    pallas_call x1, Pallas kernels, apply_experts(): pl.pallas_call(expert_block, grid=(rows // block,), in_specs=[pl.BlockSpe...  13.2 us
  transfers between devices with their start and end apart: 1, of which 0 were waited for; matrix products, arithmetic and copies ran while one was open for 2% of the time, Pallas kernels for 0%

profile of v13, /device:TPU:6, one launch (start us, length us, event | category | flops | bytes accessed | tf_op | source)
XLA Modules:
  0.0 261.5 jit_solution(3367319674717454564)
XLA Ops:
  6.5 0.0 copy-start
  6.5 0.0 all-gather.2.cloned.1.call-start
  6.5 1.6 pad_maximum_fusion
  8.1 0.0 all-gather.2.cloned.1.call-update
  8.1 0.8 select_reduce_fusion.2
  9.0 0.1 fusion.5
  9.1 1.9 select_reduce_fusion
  11.1 0.0 copy-done
  11.1 1.4 convolution_convert_fusion
  12.5 116.0 %all_to_all.10 = bf16[16,1,72,2048]{3,2,1,0:T(8,128)(2,1)} all-to-all(bf16[16,1,72,2048]{3,2,1,0:T(8,128)(2,1)S(1)} %bitcast.18), channel_id=1, replica_groups=mesh['rep'=32,'exp'=16] {'exp'}, dimensions={0} | all-to-all | bytes 9437184 | tf_op jit(solution)/shard_map/all_to_all | solution.py:67
  128.5 0.0 all-gather.2.cloned.1.call-done.gate_up_ref.down_ref
  128.5 13.2 %shard_map.73 = bf16[1152,2048]{1,0:T(8,128)(2,1)} custom-call(bf16[1152,2048]{1,0:T(8,128)(2,1)} %bitcast.19, bf16[1,2048,1152]{2,1,0:T(8,128)(2,1)} %all-gather.2.cloned.1.call-done.gate_up_ref.down_ref, bf16[1,2048,1152]{2,1,0:T(8,128)(2,1)} %all-gather.2.cloned.1.call-done.gate_up_ref.down_ref), custom_call_target="tpu_custom_call" | custom-call | tf_op jit(solution)/shard_map/pallas_call | solution.py:27
  141.7 110.4 %all_to_all.11 = bf16[16,1,72,2048]{3,2,1,0:T(8,128)(2,1)S(1)} all-to-all(bf16[16,1,72,2048]{3,2,1,0:T(8,128)(2,1)} %bitcast.20), channel_id=1, replica_groups=mesh['rep'=32,'exp'=16] {'exp'}, dimensions={0} | all-to-all | bytes 9437184 | tf_op jit(solution)/shard_map/all_to_all | solution.py:68
  252.1 0.9 fusion.3
  253.0 1.7 fusion
  (3 shorter events, 0.1 us)
Async XLA Ops:
  6.5 4.5 %copy-start = (bf16[128,2048]{1,0:T(8,128)(2,1)S(1)}, bf16[128,2048]{1,0:T(8,128)(2,1)}, u32[]{:S(2)}) copy-start(bf16[128,2048]{1,0:T(8,128)(2,1)} %param.7) | copy-start | bytes 1572868
  6.5 121.9 %all-gather.2.cloned.1.call-start = ((), (), s32[]{:S(2)}) async-start(), calls=%async_computation.2 | async-start | bytes 4866048 | tf_op jit(solution)/shard_map/all_gather | solution.py:66
Sparse Core Ops, SparseCore 0:
  10.5 93.1 all-gather.1

commit v14 on v7

--- a/solution.py
+++ b/solution.py
@@ -1,5 +1,6 @@
 import jax
 import jax.numpy as jnp
+import numpy as np
 from jax import lax
 from jax.sharding import PartitionSpec as P
 
@@ -28,14 +29,14 @@
     groups = lax.axis_size("exp")
     slots_total = experts * CAP
     expert_range = jnp.arange(experts, dtype=jnp.int32)
-    slot_ids = jnp.sum(jnp.where(expert_ids[:, :, None] == expert_range, placement_map, 0), axis=2)
-    slot_hot = slot_ids[:, :, None] == expert_range
+    holder = jnp.sum(jnp.where(placement_map[:, None] == expert_range, expert_range[:, None], 0), axis=0)
+    slot_hot = expert_ids[:, :, None] == holder
     token_hot = jnp.sum(slot_hot.astype(jnp.float32), axis=1).astype(jnp.bfloat16)
     row_range = jnp.arange(tok_rows, dtype=jnp.int32)
     earlier = (row_range[None, :] < row_range[:, None]).astype(jnp.bfloat16)
     before = jnp.dot(earlier, token_hot, preferred_element_type=jnp.float32)
-    position = jnp.sum(jnp.where(slot_hot, before[:, None, :], 0.0), axis=2).astype(jnp.int32)
-    target = slot_ids * CAP + position
+    slot_base = np.arange(experts, dtype=np.float32) * CAP
+    target = jnp.sum(jnp.where(slot_hot, before[:, None, :] + slot_base, 0.0), axis=2).astype(jnp.int32)
     slot_range = jnp.arange(slots_total, dtype=jnp.int32)
     hits = target.T[:, :, None] == slot_range
     scatter = jnp.sum(hits.astype(jnp.float32), axis=0).astype(jnp.bfloat16)

time: 260 us -> 262 us (level)
  no operation moved by 1% of the time
where the time goes in v14:
time: 262 us
  blocking collectives  226 us (86%)
  matrix products  15.6 us (6%)
  between operations  13.5 us (5%)
  other arithmetic  5.84 us (2%)
    all_to_all x1, blocking collectives, on_device(): lax.all_to_all(outgoing, 'exp', split_axis=0, concat_axis=0, tiled=True)  116 us
    all_to_all x1, blocking collectives, on_device(): lax.all_to_all(apply_experts(received, stacked), 'exp', split_axis=0, con...  110 us
  transfers between devices with their start and end apart: 1, of which 0 were waited for; matrix products, arithmetic and copies ran while one was open for 2% of the time, Pallas kernels for 0%

profile of v14, /device:TPU:6, one launch (start us, length us, event | category | flops | bytes accessed | tf_op | source)
XLA Modules:
  0.0 261.9 jit_solution(7139093522070565372)
XLA Ops:
  6.5 0.0 copy-start
  6.5 0.0 all-gather.2.cloned.1.call-start
  6.5 1.6 pad_maximum_fusion
  8.1 0.0 all-gather.2.cloned.1.call-update
  8.1 0.7 select_reduce_fusion.1
  8.9 0.8 fusion.7
  9.7 0.8 convolution_add_fusion.1
  10.4 0.8 fusion.8
  11.3 1.9 select_reduce_fusion
  13.2 0.0 copy-done
  13.2 1.4 convolution_convert_fusion.1
  14.6 116.0 %all_to_all.10 = bf16[16,1,72,2048]{3,2,1,0:T(8,128)(2,1)} all-to-all(bf16[16,1,72,2048]{3,2,1,0:T(8,128)(2,1)S(1)} %bitcast.33), channel_id=1, replica_groups=mesh['rep'=32,'exp'=16] {'exp'}, dimensions={0} | all-to-all | bytes 9437184 | tf_op jit(solution)/shard_map/all_to_all | solution.py:49
  130.6 0.0 all-gather.2.cloned.1.call-done
  130.6 0.0 copy-start.1
  130.6 0.0 copy-start.2
  130.6 5.1 %fusion.2 = f32[1152,384]{1,0:T(8,128)S(1)} fusion(bf16[1152,2048]{1,0:T(8,128)(2,1)} %bitcast.34, bf16[3,1,2048,384]{3,2,1,0:T(8,128)(2,1)} %all-gather.2.cloned.1.call-done), kind=kOutput, calls=%fused_computation.12 | convolution fusion | flops 1811939328 | bytes 8060928 | tf_op jit(solution)/shard_map/dot_general | solution.py:13
  135.7 0.0 copy-done.1
  135.7 0.6 copy-done.2
  136.2 2.9 %fusion = bf16[1152,384]{1,0:T(8,128)(2,1)S(1)} fusion(bf16[1152,2048]{1,0:T(8,128)(2,1)S(1)} %bitcast.35, f32[1152,384]{1,0:T(8,128)S(1)} %fusion.2, bf16[3,1,2048,384]{3,2,1,0:T(8,128)(2,1)S(1)} %copy-done.2), kind=kOutput, calls=%fused_computation.6 | convolution fusion | flops 1814593536 | bytes 8945664 | tf_op jit(solution)/shard_map/dot_general | solution.py:14
  139.1 2.9 %convolution_convert_fusion = bf16[1152,2048]{1,0:T(8,128)(2,1)S(1)} fusion(bf16[1152,384]{1,0:T(8,128)(2,1)S(1)} %fusion, bf16[3,1,2048,384]{3,2,1,0:T(8,128)(2,1)S(1)} %copy-done.2), kind=kOutput, calls=%fused_computation | convolution fusion | flops 1814298624 | bytes 7176192 | tf_op jit(solution)/shard_map/dot_general | solution.py:17
  142.0 110.5 %all_to_all.11 = bf16[16,1,72,2048]{3,2,1,0:T(8,128)(2,1)S(1)} all-to-all(bf16[16,1,72,2048]{3,2,1,0:T(8,128)(2,1)S(1)} %bitcast.36), channel_id=1, replica_groups=mesh['rep'=32,'exp'=16] {'exp'}, dimensions={0} | all-to-all | bytes 9437184 | tf_op jit(solution)/shard_map/all_to_all | solution.py:50
  252.5 0.9 fusion.5
  253.4 1.7 fusion.1
  (1 shorter events, 0.0 us)
Async XLA Ops:
  6.5 6.7 %copy-start = (bf16[128,2048]{1,0:T(8,128)(2,1)S(1)}, bf16[128,2048]{1,0:T(8,128)(2,1)}, u32[]{:S(2)}) copy-start(bf16[128,2048]{1,0:T(8,128)(2,1)} %param.8) | copy-start | bytes 1572868
  6.5 124.0 %all-gather.2.cloned.1.call-start = ((), (), s32[]{:S(2)}) async-start(), calls=%async_computation.2 | async-start | bytes 4866048 | tf_op jit(solution)/shard_map/all_gather | solution.py:48
  130.6 5.1 %copy-start.1 = (bf16[16,1,72,2048]{3,2,1,0:T(8,128)(2,1)S(1)}, bf16[16,1,72,2048]{3,2,1,0:T(8,128)(2,1)}, u32[]{:S(2)}) copy-start(bf16[16,1,72,2048]{3,2,1,0:T(8,128)(2,1)} %all_to_all.10) | copy-start | bytes 14155780
  130.6 5.6 %copy-start.2 = (bf16[3,1,2048,384]{3,2,1,0:T(8,128)(2,1)S(1)}, bf16[3,1,2048,384]{3,2,1,0:T(8,128)(2,1)}, u32[]{:S(2)}) copy-start(bf16[3,1,2048,384]{3,2,1,0:T(8,128)(2,1)} %all-gather.2.cloned.1.call-done) | copy-start | bytes 14155780
Sparse Core Ops, SparseCore 0:
  10.5 94.0 all-gather.1
